TPU v7x, 128 devices: a whole 4x4x4 slice. The times are simulated.
128 devices in a mesh: gx: 32 (over y, x, core), gy: 4 (over z).
Axes of the slice: x: 4, y: 4, z: 4, core: 2. Of those that a mesh axis runs over, the one named last changes fastest.
Arguments:
- east_blocks: int32 [64, 4], P(None, 'gy'), may hold values from 0 to 2, as said below
- job_code: int32 [832, 4], P('gx', 'gy'), may hold values from -1 to 2282, as said below
- factor_panels: bfloat16 [832, 4, 2, 1536, 128], P('gx', 'gy'), as said below
- dual_rhs: float32 [64, 4, 256, 384], P('gx', 'gy'), may hold values from -6 to 6
Outputs:
- multipliers: float32 [64, 4, 256, 384], P('gx', 'gy')
- residual: float32 [64, 4, 256, 384], P('gx', 'gy')
Inputs may be any that keep to these rules, and one draw needn't show every extreme that they name: `east_blocks`: in each row sy the faces sx = s0 to s0 + 15 carry 2 blocks, for a start s0 drawn per row from 1 to 46; the other faces carry 1, and the face at sx = 63 carries 0. `job_code`: A code (sx * 6 + bi) * 6 + bj names the upper tile bi <= bj < nb of subdomain (sx, sy) for column sy. In each column the live tiles, ordered by sx, then bi, then bj, are numbered k = 0, 1, ... and sit at row (k % 32) * 26 + k // 32; all other slots hold -1. Hence one device of gx forms at most 2 tiles of the subdomains of one gx index, and exactly 2 for some. `factor_panels`: A live slot holds column blocks bi and bj of subdomain (sx, sy)'s factor of 1536 rows and 768 columns, the same block wherever it appears; empty slots hold zeros.
All inputs are finite; a program needn't handle non-finite values.
Results may differ from a plain program's by a relative error of at most 0.0059.
Values may be sent and summed in bfloat16 or wider, within the bound.
No kernel may reach another device: no remote copies, remote signals or barrier semaphores. Data moves between devices by JAX's collectives and lax.ppermute only.
A program may use at most 128 MiB of HBM per device.

v0:
```python
import jax
import jax.numpy as jnp
from jax import lax
from jax.sharding import PartitionSpec as P

NB = 6
ITERS = 4


CHEB_LOW = 0.2
CHEB_HIGH = 7.0


def from_behind(value, axis, steps):
    count = lax.axis_size(axis)
    initial, last = (max(0, -steps), min(count, count - steps))
    return lax.ppermute(value, axis, [(source, source + steps) for source in range(initial, last)])


def tile_form(upper_tiles):
    upper_f = upper_tiles.astype(jnp.float32)
    flipped = jnp.swapaxes(jnp.swapaxes(upper_f, 1, 2), 3, 4)
    block_row = jnp.arange(NB, dtype=jnp.int32)
    keep_upper = (block_row[:, None] <= block_row[None, :])[None, :, :, None, None]
    return jnp.where(keep_upper, upper_f, flipped)


def slot_sources(count_row):
    west_n = count_row[0]
    east_n = count_row[1]
    south_n = count_row[2]
    north_n = count_row[3]
    within = jnp.array([0, 1, 0, 1, 0, 0], jnp.int32)
    offsets = jnp.stack(
        [0 * west_n, 0 * west_n, west_n, west_n, west_n + east_n, west_n + east_n + south_n]
    )
    limits = jnp.stack([west_n, west_n, east_n, east_n, south_n, north_n])
    source = jnp.minimum(offsets + within, NB - 1)
    alive = (within < limits).astype(jnp.float32)
    return (source, alive)


def arranged(full_tiles, count_row):
    source, alive = slot_sources(count_row)
    picked = jnp.take(jnp.take(full_tiles, source, axis=0), source, axis=1)
    picked = picked * (alive[:, None] * alive[None, :])[:, :, None, None]
    block_len = full_tiles.shape[-1]
    return picked.transpose(0, 2, 1, 3).reshape(NB * block_len, NB * block_len)


def face_mask(counts, block_len):
    east_lane = jnp.arange(2 * block_len, dtype=jnp.int32) // block_len
    east_ok = east_lane < counts[..., 1:2]
    north_ok = jnp.zeros((block_len,), jnp.int32) < counts[..., 3:4]
    return jnp.concatenate([east_ok, north_ok], axis=-1).astype(jnp.float32)


def shards(east_blocks, job_code, factor_panels, dual_rhs):
    gx_count = lax.axis_size("gx")
    gy_count = lax.axis_size("gy")
    gx_index = lax.axis_index("gx")
    gy_index = lax.axis_index("gy")
    block_len = factor_panels.shape[-1]
    sub_count = dual_rhs.shape[0]
    column = east_blocks[:, 0]
    west_column = jnp.concatenate([jnp.zeros((1,), jnp.int32), column[:-1]])
    first_sub = gx_index * sub_count
    east_own = lax.dynamic_slice_in_dim(column, first_sub, sub_count)
    west_own = lax.dynamic_slice_in_dim(west_column, first_sub, sub_count)
    south_own = jnp.broadcast_to((gy_index > 0).astype(jnp.int32), (sub_count,))
    north_own = jnp.broadcast_to((gy_index < gy_count - 1).astype(jnp.int32), (sub_count,))
    counts = jnp.stack([west_own, east_own, south_own, north_own], axis=-1)
    tiles = jnp.einsum(
        "jka,jkb->jab",
        factor_panels[:, 0, 0],
        factor_panels[:, 0, 1],
        preferred_element_type=jnp.float32,
    ).astype(jnp.bfloat16)
    tile_codes = job_code[:, 0]
    job_count = tile_codes.shape[0]
    is_valid = tile_codes >= 0
    owner_gx = jnp.where(is_valid, tile_codes // (NB * NB) // sub_count, 0)
    slot_cap = (sub_count * NB * (NB + 1) // 2 + gx_count - 1) // gx_count
    job_order = jnp.arange(job_count, dtype=jnp.int32)
    same_owner = (
        (owner_gx[:, None] == owner_gx[None, :])
        & is_valid[None, :]
        & (job_order[None, :] < job_order[:, None])
    )
    slot_rank = jnp.sum(same_owner.astype(jnp.int32), axis=1)
    send_slot = jnp.where(is_valid, owner_gx * slot_cap + slot_rank, gx_count * slot_cap)
    send_tiles = (
        jnp.zeros((gx_count * slot_cap, block_len, block_len), jnp.bfloat16)
        .at[send_slot]
        .set(tiles, mode="drop")
    )
    send_tiles = send_tiles.reshape(gx_count, slot_cap, block_len, block_len)
    send_codes = (
        jnp.full((gx_count * slot_cap,), -1, jnp.int32).at[send_slot].set(tile_codes, mode="drop")
    )
    send_codes = send_codes.reshape(gx_count, slot_cap)
    got_tiles, got_codes = (
        lax.all_to_all(send_tiles, "gx", split_axis=0, concat_axis=0, tiled=True),
        lax.all_to_all(send_codes, "gx", split_axis=0, concat_axis=0, tiled=True),
    )
    flat_codes = got_codes.reshape(-1)
    flat_tiles = got_tiles.reshape(-1, block_len, block_len)
    local_index = jnp.where(
        flat_codes >= 0,
        flat_codes // (NB * NB) % sub_count * (NB * NB) + flat_codes % (NB * NB),
        sub_count * NB * NB,
    )
    upper_tiles = (
        jnp.zeros((sub_count * NB * NB, block_len, block_len), jnp.bfloat16)
        .at[local_index]
        .set(flat_tiles, mode="drop")
    )
    full_tiles = tile_form(upper_tiles.reshape(sub_count, NB, NB, block_len, block_len))
    matrices = jax.vmap(arranged)(full_tiles, counts)
    residual = dual_rhs[:, 0] * face_mask(counts, block_len)[:, None, :]
    cheb_center = (CHEB_HIGH + CHEB_LOW) / 2.0
    cheb_radius = (CHEB_HIGH - CHEB_LOW) / 2.0
    cheb_ratio = cheb_center / cheb_radius
    cheb_rho = 1.0 / cheb_ratio
    update = residual / cheb_center
    multipliers = jnp.zeros_like(residual)
    for sweep in range(ITERS):
        multipliers = multipliers + update
        east_part = update[..., : 2 * block_len]
        to_north_part = update[..., 2 * block_len :]
        from_west = from_behind(east_part[sub_count - 1], "gx", 1)
        from_south = from_behind(to_north_part, "gy", 1)
        west_in = -jnp.concatenate([from_west[None], east_part[: sub_count - 1]], axis=0)
        image = jnp.einsum(
            "ncm,nmk->nck",
            jnp.concatenate([west_in, east_part, -from_south, to_north_part], axis=-1),
            matrices,
            precision=lax.Precision.HIGHEST,
        )
        west_part = image[..., : 2 * block_len]
        split_east_part = image[..., 2 * block_len : 4 * block_len]
        south_part = image[..., 4 * block_len : 5 * block_len]
        split_north_part = image[..., 5 * block_len :]
        from_east = from_behind(west_part[0], "gx", -1)
        from_north = from_behind(south_part, "gy", -1)
        east_near = jnp.concatenate([west_part[1:], from_east[None]], axis=0)
        residual = residual - jnp.concatenate(
            [split_east_part - east_near, split_north_part - from_north], axis=-1
        )
        rho_next = 1.0 / (2.0 * cheb_ratio - cheb_rho)
        update = rho_next * cheb_rho * update + 2.0 * rho_next / cheb_radius * residual
        cheb_rho = rho_next
    return (multipliers[:, None], residual[:, None])


def solution(mesh):
    in_specs = (
        P(None, "gy"),
        P("gx", "gy"),
        P("gx", "gy", None, None, None),
        P("gx", "gy", None, None),
    )
    out_specs = (P("gx", "gy", None, None), P("gx", "gy", None, None))
    return jax.shard_map(shards, mesh=mesh, in_specs=in_specs, out_specs=out_specs, check_vma=False)
```

profile of v0, /device:TPU:17, one launch (start us, length us, event | category | flops | bytes accessed | tf_op | source)
XLA Modules:
  0.0 224.6 jit_solution(8553963937481376639)
XLA Ops:
  5.0 7.7 %all-to-all-start = ((s32[32,1,2]{2,1,0:T(1,128)}), s32[32,1,2]{2,1,0:T(1,128)S(1)}, u32[]{:S(2)}, u32[]{:S(2)}) async-start(s32[32,1,2]{2,1,0:T(1,128)} %bitcast.14), calls=%async_computation | async-start | bytes 32768 | tf_op jit(solution)/shard_map/all_to_all | solution.py:104
  13.4 8.7 %fusion.38 = bf16[26,128,128]{2,1,0:T(8,128)(2,1)S(1)} fusion(bf16[26,1,2,1536,128]{4,3,2,1,0:T(8,128)(2,1)} %param.7), kind=kOutput, calls=%fused_computation.46 | convolution fusion | flops 1309048832 | bytes 21299200 | tf_op jit(solution)/shard_map/jka,jkb->jab/dot_general | solution.py:73
  25.1 4.3 %scatter_fusion = bf16[64,128,128]{2,1,0:T(8,128)(2,1)} fusion(bf16[64,128,128]{2,1,0:T(8,128)(2,1)} %broadcast_in_dim.98, s32[26]{0:T(128)S(1)} %fusion.57, bf16[26,128,128]{2,1,0:T(8,128)(2,1)S(1)} %fusion.38), kind=kCustom, calls=%fused_computation.3 | custom fusion | bytes 2556008 | tf_op jit(solution)/shard_map/scatter | solution.py:95
  29.5 7.4 %all-to-all-start.1 = ((bf16[32,2,128,128]{3,2,1,0:T(8,128)(2,1)}), bf16[32,2,128,128]{3,2,1,0:T(8,128)(2,1)S(1)}, u32[]{:S(2)}, u32[]{:S(2)}) async-start(bf16[32,2,128,128]{3,2,1,0:T(8,128)(2,1)} %bitcast.18), calls=%async_computation.1 | async-start | bytes 4194304 | tf_op jit(solution)/shard_map/all_to_all | solution.py:103
  38.6 3.4 %collective-permute-start = (f32[256,256]{1,0:T(8,128)}, f32[256,256]{1,0:T(8,128)}, u32[]{:S(2)}, u32[]{:S(2)}) collective-permute-start(f32[256,256]{1,0:T(8,128)} %get-tuple-element.34), channel_id=1, source_target_pairs={{0,4},{4,8},{8,12},{12,16},{16,20},{20,24},{24,28},{28,32},{32,36}... | collective-permute-start | bytes 786440 | tf_op jit(solution)/shard_map/ppermute | solution.py:17
  43.0 4.5 %collective-permute-start.1 = (f32[2,256,128]{2,1,0:T(8,128)S(1)}, f32[2,256,128]{2,1,0:T(8,128)}, u32[]{:S(2)}, u32[]{:S(2)}) collective-permute-start(f32[2,256,128]{2,1,0:T(8,128)S(1)} %slice.187), channel_id=1, source_target_pairs={{0,1},{1,2},{2,3},{4,5},{5,6},{6,7},{8,9},{9,10},{10,11},{12,13},{... | collective-permute-start | bytes 786440 | tf_op jit(solution)/shard_map/ppermute | solution.py:17
  54.0 9.8 %collective-permute-done = f32[256,256]{1,0:T(8,128)} collective-permute-done((f32[256,256]{1,0:T(8,128)}, f32[256,256]{1,0:T(8,128)}, u32[]{:S(2)}, u32[]{:S(2)}) %collective-permute-start) | collective-permute-done | bytes 262176 | tf_op jit(solution)/shard_map/ppermute | solution.py:17
  67.5 6.7 %scatter_fusion.1 = bf16[72,128,128]{2,1,0:T(8,128)(2,1)S(1)} fusion(bf16[72,128,128]{2,1,0:T(8,128)(2,1)S(1)} %broadcast_in_dim.94, s32[64]{0:T(128)S(1)} %fusion.55, bf16[64,128,128]{2,1,0:T(8,128)(2,1)} %bitcast.150), kind=kCustom, calls=%fused_computation.4 | custom fusion | bytes 6291712 | tf_op jit(solution)/shard_map/scatter | solution.py:116
  77.2 5.6 %bitcast_select_fusion = f32[2,6,6,128,128]{4,3,2,1,0:T(8,128)} fusion(f32[2,6,6,128,128]{3,4,1,2,0:T(8,128)} %copy.53, pred[6,6]{1,0:T(8,128)(4,1)S(1)} %iota_compare_fusion.1, bf16[2,6,6,128,128]{4,3,2,1,0:T(8,128)(2,1)S(1)} %bitcast.147), kind=kLoop, calls=%fused_computation.12 | loop fusion | flops 2359296 | bytes 11796516 | tf_op jit(solution)/shard_map/jit(_where)/select_n | solution.py:25
  82.8 5.4 %gather_fusion = f32[12,6,128,128]{3,2,1,0:T(8,128)} fusion(f32[2,6,6,128,128]{4,3,2,1,0:T(8,128)} %bitcast_select_fusion, s32[12]{0:T(128)S(1)} %reshape.246), kind=kCustom, calls=%fused_computation | custom fusion | bytes 9437280 | tf_op jit(solution)/shard_map/vmap(jit(_take))/gather | solution.py:45
  88.3 5.4 %broadcast_select_fusion = f32[2,6,6,128,128]{4,3,2,1,0:T(8,128)} fusion(f32[2,6,6,128,128]{4,3,2,1,0:T(8,128)} %bitcast.148, pred[2,6]{1,0:T(4,128)(4,1)S(1)} %compare_and_fusion), kind=kLoop, calls=%fused_computation.13 | loop fusion | flops 1179648 | bytes 9437196 | tf_op jit(solution)/shard_map/vmap(jit(_take))/select_n | solution.py:45
  93.7 5.4 %gather_fusion.1 = f32[12,6,128,128]{3,2,1,0:T(8,128)} fusion(f32[2,6,6,128,128]{4,3,2,1,0:T(8,128)} %broadcast_select_fusion, s32[12]{0:T(128)S(1)} %reshape.246), kind=kCustom, calls=%fused_computation.1 | custom fusion | bytes 9437280 | tf_op jit(solution)/shard_map/vmap(jit(_take))/gather | solution.py:45
  101.9 5.5 %copy.58 = f32[2,6,128,6,128]{4,3,2,1,0:T(8,128)} copy(f32[2,6,128,6,128]{4,2,1,3,0:T(8,128)S(1)} %fusion.5) | data formatting | bytes 9437184 | tf_op jit(solution)/shard_map/vmap()/mul | solution.py:46
  107.3 7.0 %reshape.244 = f32[2,768,768]{2,1,0:T(8,128)} reshape(f32[2,6,128,6,128]{4,3,2,1,0:T(8,128)} %copy.58) | data formatting | bytes 9437184 | tf_op jit(solution)/shard_map/vmap()/reshape | solution.py:48
  114.3 6.3 %fusion.6 = f32[2,256,768]{2,1,0:T(8,128)S(1)} fusion(f32[2,768,768]{2,1,0:T(8,128)} %reshape.244, f32[2,256,128]{2,1,0:T(8,128)S(1)} %slice.187, f32[2,256,128]{2,1,0:T(8,128)S(1)} %copy-done.3, f32[2,256,256]{2,1,0:T(8,128)S(1)} %slice-done.2, f32[2,256,256]{2,1,0:T(8,128)S(1)} %copy-done.2), kind=kOutput, calls=%fused_computation.14 | convolution fusion | flops 3625058304 | bytes 7864320 | tf_op jit(solution)/shard_map/ncm,nmk->nck/dot_general | solution.py:134
  120.7 4.6 %collective-permute-start.2 = (f32[256,256]{1,0:T(8,128)S(1)}, f32[256,256]{1,0:T(8,128)S(1)}, u32[]{:S(2)}, u32[]{:S(2)}) collective-permute-start(f32[256,256]{1,0:T(8,128)S(1)} %get-tuple-element.27), channel_id=1, source_target_pairs={{4,0},{8,4},{12,8},{16,12},{20,16},{24,20},{28,24},{32,28},{36,32}... | collective-permute-start | bytes 786440 | tf_op jit(solution)/shard_map/ppermute | solution.py:17
  129.4 6.4 %collective-permute-done.3 = f32[2,256,128]{2,1,0:T(8,128)S(1)} collective-permute-done((f32[2,256,128]{2,1,0:T(8,128)S(1)}, f32[2,256,128]{2,1,0:T(8,128)S(1)}, u32[]{:S(2)}, u32[]{:S(2)}) %collective-permute-start.3) | collective-permute-done | bytes 262176 | tf_op jit(solution)/shard_map/ppermute | solution.py:17
  138.5 3.8 %collective-permute-start.5 = (f32[2,256,128]{2,1,0:T(8,128)S(1)}, f32[2,256,128]{2,1,0:T(8,128)S(1)}, u32[]{:S(2)}, u32[]{:S(2)}) collective-permute-start(f32[2,256,128]{2,1,0:T(8,128)S(1)} %slice.196), channel_id=1, source_target_pairs={{0,1},{1,2},{2,3},{4,5},{5,6},{6,7},{8,9},{9,10},{10,11},{12,13},{... | collective-permute-start | bytes 786440 | tf_op jit(solution)/shard_map/ppermute | solution.py:17
  142.3 5.2 %collective-permute-done.5 = f32[2,256,128]{2,1,0:T(8,128)S(1)} collective-permute-done((f32[2,256,128]{2,1,0:T(8,128)S(1)}, f32[2,256,128]{2,1,0:T(8,128)S(1)}, u32[]{:S(2)}, u32[]{:S(2)}) %collective-permute-start.5) | collective-permute-done | bytes 262176 | tf_op jit(solution)/shard_map/ppermute | solution.py:17
  147.6 4.2 %fusion.14 = f32[2,256,768]{2,1,0:T(8,128)S(1)} fusion(f32[2,768,768]{2,1,0:T(8,128)S(1)} %bitcast.145, f32[2,256,128]{2,1,0:T(8,128)S(1)} %slice.196, f32[2,256,128]{2,1,0:T(8,128)S(1)} %neg.27, f32[2,256,256]{2,1,0:T(8,128)S(1)} %slice.195, f32[2,256,256]{2,1,0:T(8,128)S(1)} %maximum_negate_fusion.1), kind=kOutput, calls=%fused_computation.22 | convolution fusion | flops 3625058304 | bytes 7864320 | tf_op jit(solution)/shard_map/ncm,nmk->nck/dot_general | solution.py:134
  156.0 3.5 %collective-permute-done.6 = f32[256,256]{1,0:T(8,128)S(1)} collective-permute-done((f32[256,256]{1,0:T(8,128)S(1)}, f32[256,256]{1,0:T(8,128)S(1)}, u32[]{:S(2)}, u32[]{:S(2)}) %collective-permute-start.6) | collective-permute-done | bytes 262176 | tf_op jit(solution)/shard_map/ppermute | solution.py:17
  162.8 5.8 %collective-permute-start.8 = (f32[256,256]{1,0:T(8,128)S(1)}, f32[256,256]{1,0:T(8,128)S(1)}, u32[]{:S(2)}, u32[]{:S(2)}) collective-permute-start(f32[256,256]{1,0:T(8,128)S(1)} %get-tuple-element.30), channel_id=1, source_target_pairs={{0,4},{4,8},{8,12},{12,16},{16,20},{20,24},{24,28},{28,32},{32,36}... | collective-permute-start | bytes 786440 | tf_op jit(solution)/shard_map/ppermute | solution.py:17
  168.7 3.4 %collective-permute-start.9 = (f32[2,256,128]{2,1,0:T(8,128)S(1)}, f32[2,256,128]{2,1,0:T(8,128)S(1)}, u32[]{:S(2)}, u32[]{:S(2)}) collective-permute-start(f32[2,256,128]{2,1,0:T(8,128)S(1)} %slice.205), channel_id=1, source_target_pairs={{0,1},{1,2},{2,3},{4,5},{5,6},{6,7},{8,9},{9,10},{10,11},{12,13},{... | collective-permute-start | bytes 786440 | tf_op jit(solution)/shard_map/ppermute | solution.py:17
  172.2 5.6 %collective-permute-done.9 = f32[2,256,128]{2,1,0:T(8,128)S(1)} collective-permute-done((f32[2,256,128]{2,1,0:T(8,128)S(1)}, f32[2,256,128]{2,1,0:T(8,128)S(1)}, u32[]{:S(2)}, u32[]{:S(2)}) %collective-permute-start.9) | collective-permute-done | bytes 262176 | tf_op jit(solution)/shard_map/ppermute | solution.py:17
  177.8 4.2 %fusion.22 = f32[2,256,768]{2,1,0:T(8,128)S(1)} fusion(f32[2,768,768]{2,1,0:T(8,128)S(1)} %bitcast.145, f32[2,256,128]{2,1,0:T(8,128)S(1)} %slice.205, f32[2,256,128]{2,1,0:T(8,128)S(1)} %neg.29, f32[2,256,256]{2,1,0:T(8,128)S(1)} %slice.204, f32[2,256,256]{2,1,0:T(8,128)S(1)} %maximum_negate_fusion.2), kind=kOutput, calls=%fused_computation.30 | convolution fusion | flops 3625058304 | bytes 7864320 | tf_op jit(solution)/shard_map/ncm,nmk->nck/dot_general | solution.py:134
  186.1 3.6 %collective-permute-done.10 = f32[256,256]{1,0:T(8,128)S(1)} collective-permute-done((f32[256,256]{1,0:T(8,128)S(1)}, f32[256,256]{1,0:T(8,128)S(1)}, u32[]{:S(2)}, u32[]{:S(2)}) %collective-permute-start.10) | collective-permute-done | bytes 262176 | tf_op jit(solution)/shard_map/ppermute | solution.py:17
  189.7 3.5 %collective-permute-done.11 = f32[2,256,128]{2,1,0:T(8,128)S(1)} collective-permute-done((f32[2,256,128]{2,1,0:T(8,128)S(1)}, f32[2,256,128]{2,1,0:T(8,128)S(1)}, u32[]{:S(2)}, u32[]{:S(2)}) %collective-permute-start.11) | collective-permute-done | bytes 262176 | tf_op jit(solution)/shard_map/ppermute | solution.py:17
  193.6 4.6 %collective-permute-start.12 = (f32[256,256]{1,0:T(8,128)S(1)}, f32[256,256]{1,0:T(8,128)S(1)}, u32[]{:S(2)}, u32[]{:S(2)}) collective-permute-start(f32[256,256]{1,0:T(8,128)S(1)} %get-tuple-element.28), channel_id=1, source_target_pairs={{0,4},{4,8},{8,12},{12,16},{16,20},{20,24},{24,28},{28,32},{32,36}... | collective-permute-start | bytes 786440 | tf_op jit(solution)/shard_map/ppermute | solution.py:17
  198.2 3.6 %collective-permute-start.13 = (f32[2,256,128]{2,1,0:T(8,128)S(1)}, f32[2,256,128]{2,1,0:T(8,128)S(1)}, u32[]{:S(2)}, u32[]{:S(2)}) collective-permute-start(f32[2,256,128]{2,1,0:T(8,128)S(1)} %slice.214), channel_id=1, source_target_pairs={{0,1},{1,2},{2,3},{4,5},{5,6},{6,7},{8,9},{9,10},{10,11},{12,13},{... | collective-permute-start | bytes 786440 | tf_op jit(solution)/shard_map/ppermute | solution.py:17
  202.0 5.0 %collective-permute-done.13 = f32[2,256,128]{2,1,0:T(8,128)S(1)} collective-permute-done((f32[2,256,128]{2,1,0:T(8,128)S(1)}, f32[2,256,128]{2,1,0:T(8,128)S(1)}, u32[]{:S(2)}, u32[]{:S(2)}) %collective-permute-start.13) | collective-permute-done | bytes 262176 | tf_op jit(solution)/shard_map/ppermute | solution.py:17
  207.1 4.2 %fusion.30 = f32[2,256,768]{2,1,0:T(8,128)S(1)} fusion(f32[2,768,768]{2,1,0:T(8,128)S(1)} %bitcast.145, f32[2,256,128]{2,1,0:T(8,128)S(1)} %slice.214, f32[2,256,128]{2,1,0:T(8,128)S(1)} %neg.31, f32[2,256,256]{2,1,0:T(8,128)S(1)} %slice.213, f32[2,256,256]{2,1,0:T(8,128)S(1)} %maximum_negate_fusion.3), kind=kOutput, calls=%fused_computation.38 | convolution fusion | flops 3625058304 | bytes 7864320 | tf_op jit(solution)/shard_map/ncm,nmk->nck/dot_general | solution.py:134
  219.1 3.9 %collective-permute-done.15 = f32[2,256,128]{2,1,0:T(8,128)S(1)} collective-permute-done((f32[2,256,128]{2,1,0:T(8,128)S(1)}, f32[2,256,128]{2,1,0:T(8,128)S(1)}, u32[]{:S(2)}, u32[]{:S(2)}) %collective-permute-start.15) | collective-permute-done | bytes 262176 | tf_op jit(solution)/shard_map/ppermute | solution.py:17
  (120 shorter events, 55.2 us)
Async XLA Ops:
  5.0 24.4 %all-to-all-start = ((s32[32,1,2]{2,1,0:T(1,128)}), s32[32,1,2]{2,1,0:T(1,128)S(1)}, u32[]{:S(2)}, u32[]{:S(2)}) async-start(s32[32,1,2]{2,1,0:T(1,128)} %bitcast.14), calls=%async_computation | async-start | bytes 32768 | tf_op jit(solution)/shard_map/all_to_all | solution.py:104
  13.4 8.8 %copy-start.5 = (s32[64,1]{0,1:T(1,128)S(1)}, s32[64,1]{0,1:T(1,128)}, u32[]{:S(2)}) copy-start(s32[64,1]{0,1:T(1,128)} %param.5) | copy-start | bytes 772
  13.4 8.9 %copy-start = (f32[2,1,256,384]{3,2,1,0:T(8,128)S(1)}, f32[2,1,256,384]{3,2,1,0:T(8,128)}, u32[]{:S(2)}) copy-start(f32[2,1,256,384]{3,2,1,0:T(8,128)} %param.8) | copy-start | bytes 2359300
  29.5 36.1 %all-to-all-start.1 = ((bf16[32,2,128,128]{3,2,1,0:T(8,128)(2,1)}), bf16[32,2,128,128]{3,2,1,0:T(8,128)(2,1)S(1)}, u32[]{:S(2)}, u32[]{:S(2)}) async-start(bf16[32,2,128,128]{3,2,1,0:T(8,128)(2,1)} %bitcast.18), calls=%async_computation.1 | async-start | bytes 4194304 | tf_op jit(solution)/shard_map/all_to_all | solution.py:103
  36.9 11.1 %copy-start.4 = (s32[6]{0:T(128)S(1)}, s32[6]{0:T(128)}, u32[]{:S(2)}) copy-start(s32[6]{0:T(128)} %constant.135.clone) | copy-start | bytes 76
  38.6 25.1 %collective-permute-start = (f32[256,256]{1,0:T(8,128)}, f32[256,256]{1,0:T(8,128)}, u32[]{:S(2)}, u32[]{:S(2)}) collective-permute-start(f32[256,256]{1,0:T(8,128)} %get-tuple-element.34), channel_id=1, source_target_pairs={{0,4},{4,8},{8,12},{12,16},{16,20},{20,24},{24,28},{28,32},{32,36}... | collective-permute-start | bytes 786440 | tf_op jit(solution)/shard_map/ppermute | solution.py:17
  43.0 9.4 %collective-permute-start.1 = (f32[2,256,128]{2,1,0:T(8,128)S(1)}, f32[2,256,128]{2,1,0:T(8,128)}, u32[]{:S(2)}, u32[]{:S(2)}) collective-permute-start(f32[2,256,128]{2,1,0:T(8,128)S(1)} %slice.187), channel_id=1, source_target_pairs={{0,1},{1,2},{2,3},{4,5},{5,6},{6,7},{8,9},{9,10},{10,11},{12,13},{... | collective-permute-start | bytes 786440 | tf_op jit(solution)/shard_map/ppermute | solution.py:17
  65.6 1.3 copy-start.1
  107.3 7.0 %slice-start.2 = ((f32[2,256,384]{2,1,0:T(8,128)}), f32[2,256,256]{2,1,0:T(8,128)S(1)}, s32[]{:S(2)}) async-start(f32[2,256,384]{2,1,0:T(8,128)} %fusion.46), calls=%async_computation.4 | async-start | bytes 1048576 | tf_op jit(solution)/shard_map/slice | solution.py:129
  107.3 7.0 %copy-start.2 = (f32[2,256,256]{2,1,0:T(8,128)S(1)}, f32[2,256,256]{2,1,0:T(8,128)}, u32[]{:S(2)}) copy-start(f32[2,256,256]{2,1,0:T(8,128)} %maximum_negate_fusion) | copy-start | bytes 1572868
  107.3 7.0 %copy-start.3 = (f32[2,256,128]{2,1,0:T(8,128)S(1)}, f32[2,256,128]{2,1,0:T(8,128)}, u32[]{:S(2)}) copy-start(f32[2,256,128]{2,1,0:T(8,128)} %neg.25) | copy-start | bytes 786436
  114.3 33.2 %slice-start = ((s8[4718592]{0:T(1024)(128)(4,1)}), s8[4194304]{0:T(1024)(128)(4,1)S(1)}, s32[]{:S(2)}) async-start(s8[4718592]{0:T(1024)(128)(4,1)} %bitcast.144), calls=%async_computation.2 | async-start | bytes 8388608
  120.7 26.8 %slice-start.1 = ((s8[4718592]{0:T(1024)(128)(4,1)}), s8[524288]{0:T(1024)(128)(4,1)S(1)}, s32[]{:S(2)}) async-start(s8[4718592]{0:T(1024)(128)(4,1)} %bitcast.144), calls=%async_computation.3 | async-start | bytes 1048576
  120.7 8.6 %collective-permute-start.2 = (f32[256,256]{1,0:T(8,128)S(1)}, f32[256,256]{1,0:T(8,128)S(1)}, u32[]{:S(2)}, u32[]{:S(2)}) collective-permute-start(f32[256,256]{1,0:T(8,128)S(1)} %get-tuple-element.27), channel_id=1, source_target_pairs={{4,0},{8,4},{12,8},{16,12},{20,16},{24,20},{28,24},{32,28},{36,32}... | collective-permute-start | bytes 786440 | tf_op jit(solution)/shard_map/ppermute | solution.py:17
  125.4 10.4 %collective-permute-start.3 = (f32[2,256,128]{2,1,0:T(8,128)S(1)}, f32[2,256,128]{2,1,0:T(8,128)S(1)}, u32[]{:S(2)}, u32[]{:S(2)}) collective-permute-start(f32[2,256,128]{2,1,0:T(8,128)S(1)} %slice.192), channel_id=1, source_target_pairs={{1,0},{2,1},{3,2},{5,4},{6,5},{7,6},{9,8},{10,9},{11,10},{13,12},{... | collective-permute-start | bytes 786440 | tf_op jit(solution)/shard_map/ppermute | solution.py:17
  136.0 6.3 %collective-permute-start.4 = (f32[256,256]{1,0:T(8,128)S(1)}, f32[256,256]{1,0:T(8,128)S(1)}, u32[]{:S(2)}, u32[]{:S(2)}) collective-permute-start(f32[256,256]{1,0:T(8,128)S(1)} %get-tuple-element.32), channel_id=1, source_target_pairs={{0,4},{4,8},{8,12},{12,16},{16,20},{20,24},{24,28},{28,32},{32,36}... | collective-permute-start | bytes 786440 | tf_op jit(solution)/shard_map/ppermute | solution.py:17
  138.5 9.1 %collective-permute-start.5 = (f32[2,256,128]{2,1,0:T(8,128)S(1)}, f32[2,256,128]{2,1,0:T(8,128)S(1)}, u32[]{:S(2)}, u32[]{:S(2)}) collective-permute-start(f32[2,256,128]{2,1,0:T(8,128)S(1)} %slice.196), channel_id=1, source_target_pairs={{0,1},{1,2},{2,3},{4,5},{5,6},{6,7},{8,9},{9,10},{10,11},{12,13},{... | collective-permute-start | bytes 786440 | tf_op jit(solution)/shard_map/ppermute | solution.py:17
  151.8 7.7 %collective-permute-start.6 = (f32[256,256]{1,0:T(8,128)S(1)}, f32[256,256]{1,0:T(8,128)S(1)}, u32[]{:S(2)}, u32[]{:S(2)}) collective-permute-start(f32[256,256]{1,0:T(8,128)S(1)} %get-tuple-element.25), channel_id=1, source_target_pairs={{4,0},{8,4},{12,8},{16,12},{20,16},{24,20},{28,24},{32,28},{36,32}... | collective-permute-start | bytes 786440 | tf_op jit(solution)/shard_map/ppermute | solution.py:17
  154.7 7.9 %collective-permute-start.7 = (f32[2,256,128]{2,1,0:T(8,128)S(1)}, f32[2,256,128]{2,1,0:T(8,128)S(1)}, u32[]{:S(2)}, u32[]{:S(2)}) collective-permute-start(f32[2,256,128]{2,1,0:T(8,128)S(1)} %slice.201), channel_id=1, source_target_pairs={{1,0},{2,1},{3,2},{5,4},{6,5},{7,6},{9,8},{10,9},{11,10},{13,12},{... | collective-permute-start | bytes 786440 | tf_op jit(solution)/shard_map/ppermute | solution.py:17
  162.8 9.3 %collective-permute-start.8 = (f32[256,256]{1,0:T(8,128)S(1)}, f32[256,256]{1,0:T(8,128)S(1)}, u32[]{:S(2)}, u32[]{:S(2)}) collective-permute-start(f32[256,256]{1,0:T(8,128)S(1)} %get-tuple-element.30), channel_id=1, source_target_pairs={{0,4},{4,8},{8,12},{12,16},{16,20},{20,24},{24,28},{28,32},{32,36}... | collective-permute-start | bytes 786440 | tf_op jit(solution)/shard_map/ppermute | solution.py:17
  168.7 9.0 %collective-permute-start.9 = (f32[2,256,128]{2,1,0:T(8,128)S(1)}, f32[2,256,128]{2,1,0:T(8,128)S(1)}, u32[]{:S(2)}, u32[]{:S(2)}) collective-permute-start(f32[2,256,128]{2,1,0:T(8,128)S(1)} %slice.205), channel_id=1, source_target_pairs={{0,1},{1,2},{2,3},{4,5},{5,6},{6,7},{8,9},{9,10},{10,11},{12,13},{... | collective-permute-start | bytes 786440 | tf_op jit(solution)/shard_map/ppermute | solution.py:17
  182.0 7.7 %collective-permute-start.10 = (f32[256,256]{1,0:T(8,128)S(1)}, f32[256,256]{1,0:T(8,128)S(1)}, u32[]{:S(2)}, u32[]{:S(2)}) collective-permute-start(f32[256,256]{1,0:T(8,128)S(1)} %get-tuple-element.23), channel_id=1, source_target_pairs={{4,0},{8,4},{12,8},{16,12},{20,16},{24,20},{28,24},{32,28},{36,32}... | collective-permute-start | bytes 786440 | tf_op jit(solution)/shard_map/ppermute | solution.py:17
  184.8 8.5 %collective-permute-start.11 = (f32[2,256,128]{2,1,0:T(8,128)S(1)}, f32[2,256,128]{2,1,0:T(8,128)S(1)}, u32[]{:S(2)}, u32[]{:S(2)}) collective-permute-start(f32[2,256,128]{2,1,0:T(8,128)S(1)} %slice.210), channel_id=1, source_target_pairs={{1,0},{2,1},{3,2},{5,4},{6,5},{7,6},{9,8},{10,9},{11,10},{13,12},{... | collective-permute-start | bytes 786440 | tf_op jit(solution)/shard_map/ppermute | solution.py:17
  193.6 8.4 %collective-permute-start.12 = (f32[256,256]{1,0:T(8,128)S(1)}, f32[256,256]{1,0:T(8,128)S(1)}, u32[]{:S(2)}, u32[]{:S(2)}) collective-permute-start(f32[256,256]{1,0:T(8,128)S(1)} %get-tuple-element.28), channel_id=1, source_target_pairs={{0,4},{4,8},{8,12},{12,16},{16,20},{20,24},{24,28},{28,32},{32,36}... | collective-permute-start | bytes 786440 | tf_op jit(solution)/shard_map/ppermute | solution.py:17
  198.2 8.9 %collective-permute-start.13 = (f32[2,256,128]{2,1,0:T(8,128)S(1)}, f32[2,256,128]{2,1,0:T(8,128)S(1)}, u32[]{:S(2)}, u32[]{:S(2)}) collective-permute-start(f32[2,256,128]{2,1,0:T(8,128)S(1)} %slice.214), channel_id=1, source_target_pairs={{0,1},{1,2},{2,3},{4,5},{5,6},{6,7},{8,9},{9,10},{10,11},{12,13},{... | collective-permute-start | bytes 786440 | tf_op jit(solution)/shard_map/ppermute | solution.py:17
  211.3 7.7 %collective-permute-start.14 = (f32[256,256]{1,0:T(8,128)S(1)}, f32[256,256]{1,0:T(8,128)S(1)}, u32[]{:S(2)}, u32[]{:S(2)}) collective-permute-start(f32[256,256]{1,0:T(8,128)S(1)} %get-tuple-element.21), channel_id=1, source_target_pairs={{4,0},{8,4},{12,8},{16,12},{20,16},{24,20},{28,24},{32,28},{36,32}... | collective-permute-start | bytes 786440 | tf_op jit(solution)/shard_map/ppermute | solution.py:17
  214.3 8.6 %collective-permute-start.15 = (f32[2,256,128]{2,1,0:T(8,128)S(1)}, f32[2,256,128]{2,1,0:T(8,128)S(1)}, u32[]{:S(2)}, u32[]{:S(2)}) collective-permute-start(f32[2,256,128]{2,1,0:T(8,128)S(1)} %slice.219), channel_id=1, source_target_pairs={{1,0},{2,1},{3,2},{5,4},{6,5},{7,6},{9,8},{10,9},{11,10},{13,12},{... | collective-permute-start | bytes 786440 | tf_op jit(solution)/shard_map/ppermute | solution.py:17
where the time goes:
time: 228 us; the launch traced here: 225 us
  starting transfers between devices  64.9 us (28%)
  waiting for transfers between devices  58.6 us (26%)
  local copies, waits for them, and re-layouts  47.7 us (21%)
  matrix products  27.5 us (12%)
  other arithmetic  24.6 us (11%)
    ppermute x16, waiting for transfers between devices, from_behind(): lax.ppermute(value, axis, [(source, source + steps) for source in range(i...  58.6 us
    ppermute x16, starting transfers between devices, from_behind(): lax.ppermute(value, axis, [(source, source + steps) for source in range(i...  49.8 us
    dot_general x4, matrix products, shards(): jnp.einsum('ncm,nmk->nck', jnp.concatenate([west_in, east_part, -from_sou...  18.8 us
    gather x3, local copies, waits for them, and re-layouts, arranged(): picked = jnp.take(jnp.take(full_tiles, source, axis=0), source, axis=1)  11 us
    dot_general x1, matrix products, shards(): jnp.einsum('jka,jkb->jab', factor_panels[:, 0, 0], factor_panels[:, 0, 1]...  8.66 us
    all_to_all x1, starting transfers between devices, shards(): lax.all_to_all(send_codes, 'gx', split_axis=0, concat_axis=0, tiled=True)  7.71 us
    all_to_all x1, starting transfers between devices, shards(): lax.all_to_all(send_tiles, 'gx', split_axis=0, concat_axis=0, tiled=True)  7.37 us
    reshape x1, local copies, waits for them, and re-layouts, arranged(): return picked.transpose(0, 2, 1, 3).reshape(NB * block_len, NB * block_len)  6.98 us
  transfers between devices with their start and end apart: 18, of which 13 were waited for; matrix products, arithmetic and copies ran while one was open for 11% of the time, Pallas kernels for 0%

commit v1 on v0

v1 whole, which is shorter than its diff:
```python
import jax
import jax.numpy as jnp
from jax import lax
from jax.sharding import PartitionSpec as P

NB = 6
ITERS = 4


CHEB_LOW = 0.2
CHEB_HIGH = 7.0


def from_behind(value, axis, steps):
    count = lax.axis_size(axis)
    initial, last = (max(0, -steps), min(count, count - steps))
    return lax.ppermute(value, axis, [(source, source + steps) for source in range(initial, last)])


def face_mask(counts, block_len):
    east_lane = jnp.arange(2 * block_len, dtype=jnp.int32) // block_len
    east_ok = east_lane < counts[..., 1:2]
    north_ok = jnp.zeros((block_len,), jnp.int32) < counts[..., 3:4]
    return jnp.concatenate([east_ok, north_ok], axis=-1).astype(jnp.float32)


def logical_slots(counts):
    west_n = counts[:, 0:1]
    east_n = counts[:, 1:2]
    south_n = counts[:, 2:3]
    north_n = counts[:, 3:4]
    within = jnp.array([0, 1, 0, 1, 0, 0], jnp.int32)[None, :]
    zero = jnp.zeros_like(west_n)
    offsets = jnp.concatenate(
        [zero, zero, west_n, west_n, west_n + east_n, west_n + east_n + south_n], axis=1
    )
    limits = jnp.concatenate([west_n, west_n, east_n, east_n, south_n, north_n], axis=1)
    return offsets + within, within < limits


def shards(east_blocks, job_code, factor_panels, dual_rhs):
    gx_count = lax.axis_size("gx")
    gy_count = lax.axis_size("gy")
    gx_index = lax.axis_index("gx")
    gy_index = lax.axis_index("gy")
    block_len = factor_panels.shape[-1]
    sub_count = dual_rhs.shape[0]
    column = east_blocks[:, 0]
    west_column = jnp.concatenate([jnp.zeros((1,), jnp.int32), column[:-1]])
    south_one = (gy_index > 0).astype(jnp.int32)
    north_one = (gy_index < gy_count - 1).astype(jnp.int32)
    blocks_all = west_column + column + south_one + north_one
    tiles_all = blocks_all * (blocks_all + 1) // 2
    first_tile_all = jnp.cumsum(tiles_all) - tiles_all
    first_sub = gx_index * sub_count
    east_own = lax.dynamic_slice_in_dim(column, first_sub, sub_count)
    west_own = lax.dynamic_slice_in_dim(west_column, first_sub, sub_count)
    blocks_own = lax.dynamic_slice_in_dim(blocks_all, first_sub, sub_count)
    first_tile_own = lax.dynamic_slice_in_dim(first_tile_all, first_sub, sub_count)
    south_own = jnp.broadcast_to(south_one, (sub_count,))
    north_own = jnp.broadcast_to(north_one, (sub_count,))
    counts = jnp.stack([west_own, east_own, south_own, north_own], axis=-1)

    tiles = jnp.einsum(
        "jka,jkb->jab",
        factor_panels[:, 0, 0],
        factor_panels[:, 0, 1],
        preferred_element_type=jnp.float32,
    ).astype(jnp.bfloat16)
    tile_codes = job_code[:, 0]
    job_count = tile_codes.shape[0]
    is_valid = tile_codes >= 0
    owner_gx = jnp.where(is_valid, tile_codes // (NB * NB) // sub_count, 0)
    slot_cap = (sub_count * NB * (NB + 1) // 2 + gx_count - 1) // gx_count
    job_order = jnp.arange(job_count, dtype=jnp.int32)
    same_owner = (
        (owner_gx[:, None] == owner_gx[None, :])
        & is_valid[None, :]
        & (job_order[None, :] < job_order[:, None])
    )
    slot_rank = jnp.sum(same_owner.astype(jnp.int32), axis=1)
    send_slot = jnp.where(is_valid & (slot_rank < slot_cap), owner_gx * slot_cap + slot_rank, -1)
    slot_count = gx_count * slot_cap
    pick_send = (
        send_slot[None, :] == jnp.arange(slot_count, dtype=jnp.int32)[:, None]
    ).astype(jnp.bfloat16)
    send_tiles = jnp.einsum(
        "mj,jab->mab", pick_send, tiles, preferred_element_type=jnp.float32
    ).astype(jnp.bfloat16)
    send_tiles = send_tiles.reshape(gx_count, slot_cap, block_len, block_len)
    got_tiles = lax.all_to_all(send_tiles, "gx", split_axis=0, concat_axis=0, tiled=True)
    got_tiles = got_tiles.reshape(slot_count, block_len, block_len)

    source, alive = logical_slots(counts)
    row_slot = source[:, :, None]
    col_slot = source[:, None, :]
    low_slot = jnp.minimum(row_slot, col_slot)
    high_slot = jnp.maximum(row_slot, col_slot)
    nb = blocks_own[:, None, None]
    pair_index = low_slot * nb - low_slot * (low_slot - 1) // 2 + (high_slot - low_slot)
    tile_number = first_tile_own[:, None, None] + pair_index
    local_number = tile_number - first_tile_own[0]
    got_slot = tile_number % gx_count * slot_cap + local_number // gx_count
    both_alive = alive[:, :, None] & alive[:, None, :]
    slot_ids = jnp.arange(slot_count, dtype=jnp.int32)
    hits = got_slot[..., None] == slot_ids
    pick_upper = (hits & (both_alive & (row_slot <= col_slot))[..., None]).astype(jnp.bfloat16)
    pick_lower = (hits & (both_alive & (row_slot > col_slot))[..., None]).astype(jnp.bfloat16)
    matrices = jnp.einsum(
        "spqf,fab->spaqb", pick_upper, got_tiles, preferred_element_type=jnp.float32
    ) + jnp.einsum(
        "spqf,fba->spaqb", pick_lower, got_tiles, preferred_element_type=jnp.float32
    )
    matrices = matrices.astype(jnp.bfloat16).reshape(sub_count, NB * block_len, NB * block_len)

    residual = dual_rhs[:, 0] * face_mask(counts, block_len)[:, None, :]
    cases = residual.shape[1]
    cheb_center = (CHEB_HIGH + CHEB_LOW) / 2.0
    cheb_radius = (CHEB_HIGH - CHEB_LOW) / 2.0
    cheb_ratio = cheb_center / cheb_radius
    cheb_rho = 1.0 / cheb_ratio
    update = residual / cheb_center
    multipliers = jnp.zeros_like(residual)
    for sweep in range(ITERS):
        multipliers = multipliers + update
        east_part = update[..., : 2 * block_len]
        to_north_part = update[..., 2 * block_len :]
        from_west = from_behind(east_part[sub_count - 1], "gx", 1)
        from_south = from_behind(to_north_part, "gy", 1)
        west_in = -jnp.concatenate([from_west[None], east_part[: sub_count - 1]], axis=0)
        local_vec = jnp.concatenate([west_in, east_part, -from_south, to_north_part], axis=-1)
        high = local_vec.astype(jnp.bfloat16)
        low = (local_vec - high.astype(jnp.float32)).astype(jnp.bfloat16)
        both = jnp.einsum(
            "ncm,nmk->nck",
            jnp.concatenate([high, low], axis=1),
            matrices,
            preferred_element_type=jnp.float32,
        )
        image = both[:, :cases] + both[:, cases:]
        west_part = image[..., : 2 * block_len]
        split_east_part = image[..., 2 * block_len : 4 * block_len]
        south_part = image[..., 4 * block_len : 5 * block_len]
        split_north_part = image[..., 5 * block_len :]
        from_east = from_behind(west_part[0], "gx", -1)
        from_north = from_behind(south_part, "gy", -1)
        east_near = jnp.concatenate([west_part[1:], from_east[None]], axis=0)
        residual = residual - jnp.concatenate(
            [split_east_part - east_near, split_north_part - from_north], axis=-1
        )
        rho_next = 1.0 / (2.0 * cheb_ratio - cheb_rho)
        update = rho_next * cheb_rho * update + 2.0 * rho_next / cheb_radius * residual
        cheb_rho = rho_next
    return (multipliers[:, None], residual[:, None])


def solution(mesh):
    in_specs = (
        P(None, "gy"),
        P("gx", "gy"),
        P("gx", "gy", None, None, None),
        P("gx", "gy", None, None),
    )
    out_specs = (P("gx", "gy", None, None), P("gx", "gy", None, None))
    return jax.shard_map(shards, mesh=mesh, in_specs=in_specs, out_specs=out_specs, check_vma=False)
```

time: 228 us -> 172 us (0.75)
  local copies, waits for them, and re-layouts: 47.7 us -> 18.9 us
  other arithmetic: 24.6 us -> 9.33 us
  matrix products: 27.5 us -> 19.3 us
  starting transfers between devices: 64.9 us -> 57.1 us
  waiting for transfers between devices: 58.6 us -> 62.8 us
    scatter x3 -> x0, local copies, waits for them, and re-layouts: 11.8 us -> none  [the longest x1 6.67 us: shards(): upper_tiles = jnp.zeros((sub_count * NB * NB, block_len, block_len), jnp....]
    select_n x4 -> x2, other arithmetic: 11.8 us -> 0.11 us  [the longest x1 0.09 us: shards(): tiles_all = blocks_all * (blocks_all + 1) // 2]
    gather x3 -> x0, local copies, waits for them, and re-layouts: 11 us -> none  [arranged(): picked = jnp.take(jnp.take(full_tiles, source, axis=0), source, axis=1)]
    dot_general x4 -> x7, matrix products: 18.8 us -> 10.6 us  [the longest x4 7.7 us: shards(): jnp.einsum('ncm,nmk->nck', jnp.concatenate([high, low], axis=1), matrices...]
    all_to_all x1 -> x0, starting transfers between devices: 7.71 us -> none  [shards(): lax.all_to_all(send_codes, 'gx', split_axis=0, concat_axis=0, tiled=True)]
    mul x1 -> x0, local copies, waits for them, and re-layouts: 5.46 us -> none  [arranged(): picked = picked * (alive[:, None] * alive[None, :])[:, :, None, None]]
    ppermute x16, waiting for transfers between devices: 58.6 us -> 62.8 us  [from_behind(): lax.ppermute(value, axis, [(source, source + steps) for source in range(i...]
    reshape x1 -> x3, local copies, waits for them, and re-layouts: 6.98 us -> 10.6 us  [the longest x1 3.71 us: shards(): matrices.astype(jnp.bfloat16)]
  transfers between devices with their start and end apart: 18 -> 17, of which waited for: 13 -> 13; matrix products, arithmetic and copies ran while one was open for 11% -> 3% of each run, Pallas kernels for 0% -> 0%
where the time goes in v1:
time: 172 us; the launch traced here: 169 us
  waiting for transfers between devices  62.8 us (37%)
  starting transfers between devices  57.1 us (33%)
  matrix products  19.3 us (11%)
  local copies, waits for them, and re-layouts  18.9 us (11%)
  other arithmetic  9.33 us (5%)
    ppermute x16, waiting for transfers between devices, from_behind(): lax.ppermute(value, axis, [(source, source + steps) for source in range(i...  62.8 us
    ppermute x16, starting transfers between devices, from_behind(): lax.ppermute(value, axis, [(source, source + steps) for source in range(i...  49.2 us
    dot_general x1, matrix products, shards(): jnp.einsum('jka,jkb->jab', factor_panels[:, 0, 0], factor_panels[:, 0, 1]...  8.61 us
    all_to_all x1, starting transfers between devices, shards(): lax.all_to_all(send_tiles, 'gx', split_axis=0, concat_axis=0, tiled=True)  7.9 us
    dot_general x4, matrix products, shards(): jnp.einsum('ncm,nmk->nck', jnp.concatenate([high, low], axis=1), matrices...  7.7 us
    all_to_all x1, local copies, waits for them, and re-layouts, shards(): lax.all_to_all(send_tiles, 'gx', split_axis=0, concat_axis=0, tiled=True)  3.95 us
    reshape x1, local copies, waits for them, and re-layouts, shards(): matrices.astype(jnp.bfloat16)  3.71 us
    reshape x1, local copies, waits for them, and re-layouts, shards(): send_tiles = send_tiles.reshape(gx_count, slot_cap, block_len, block_len)  3.52 us
  transfers between devices with their start and end apart: 17, of which 13 were waited for; matrix products, arithmetic and copies ran while one was open for 3% of the time, Pallas kernels for 0%

profile of v1, /device:TPU:17, one launch (start us, length us, event | category | flops | bytes accessed | tf_op | source)
XLA Modules:
  0.0 168.7 jit_solution(5540516198677024874)
XLA Ops:
  2.7 8.6 %fusion.22 = bf16[26,128,128]{2,1,0:T(8,128)(2,1)S(1)} fusion(bf16[26,1,2,1536,128]{4,3,2,1,0:T(8,128)(2,1)} %param.7), kind=kOutput, calls=%fused_computation.36 | convolution fusion | flops 1309048832 | bytes 21299200 | tf_op jit(solution)/shard_map/jka,jkb->jab/dot_general | solution.py:64
  12.4 3.5 %copy.50 = bf16[32,2,128,128]{3,1,2,0:T(2,128)(2,1)} copy(bf16[32,2,128,128]{3,1,0,2:T(2,128)(2,1)S(1)} %bitcast.153) | data formatting | bytes 4194304 | tf_op jit(solution)/shard_map/reshape | solution.py:90
  15.9 7.9 %all-to-all-start = ((bf16[32,2,128,128]{3,1,2,0:T(2,128)(2,1)}), bf16[32,2,128,128]{3,1,2,0:T(2,128)(2,1)}, u32[]{:S(2)}, u32[]{:S(2)}) async-start(bf16[32,2,128,128]{3,1,2,0:T(2,128)(2,1)} %copy.50), calls=%async_computation | async-start | bytes 4194304 | tf_op jit(solution)/shard_map/all_to_all | solution.py:91
  24.7 3.4 %collective-permute-start = (f32[256,256]{1,0:T(8,128)S(1)}, f32[256,256]{1,0:T(8,128)S(1)}, u32[]{:S(2)}, u32[]{:S(2)}) collective-permute-start(f32[256,256]{1,0:T(8,128)S(1)} %get-tuple-element.34), channel_id=1, source_target_pairs={{0,4},{4,8},{8,12},{12,16},{16,20},{20,24},{24,28},{28,32},{32,36}... | collective-permute-start | bytes 786440 | tf_op jit(solution)/shard_map/ppermute | solution.py:17
  28.1 3.7 %collective-permute-start.1 = (f32[2,256,128]{2,1,0:T(8,128)S(1)}, f32[2,256,128]{2,1,0:T(8,128)S(1)}, u32[]{:S(2)}, u32[]{:S(2)}) collective-permute-start(f32[2,256,128]{2,1,0:T(8,128)S(1)} %slice.219), channel_id=1, source_target_pairs={{0,1},{1,2},{2,3},{4,5},{5,6},{6,7},{8,9},{9,10},{10,11},{12,13},{... | collective-permute-start | bytes 786440 | tf_op jit(solution)/shard_map/ppermute | solution.py:17
  32.8 4.4 %collective-permute-done.1 = f32[2,256,128]{2,1,0:T(8,128)S(1)} collective-permute-done((f32[2,256,128]{2,1,0:T(8,128)S(1)}, f32[2,256,128]{2,1,0:T(8,128)S(1)}, u32[]{:S(2)}, u32[]{:S(2)}) %collective-permute-start.1) | collective-permute-done | bytes 262176 | tf_op jit(solution)/shard_map/ppermute | solution.py:17
  37.3 13.3 %collective-permute-done = f32[256,256]{1,0:T(8,128)S(1)} collective-permute-done((f32[256,256]{1,0:T(8,128)S(1)}, f32[256,256]{1,0:T(8,128)S(1)}, u32[]{:S(2)}, u32[]{:S(2)}) %collective-permute-start) | collective-permute-done | bytes 262176 | tf_op jit(solution)/shard_map/ppermute | solution.py:17
  52.6 3.9 %copy.51 = bf16[32,2,128,128]{3,1,0,2:T(2,128)(2,1)S(1)} copy(bf16[32,2,128,128]{3,1,2,0:T(2,128)(2,1)} %all-to-all-done) | data formatting | bytes 4194304 | tf_op jit(solution)/shard_map/all_to_all | solution.py:91
  56.6 3.4 %copy.67 = bf16[64,128,128,1,1]{1,0,4,3,2:T(8,128)(2,1)} copy(bf16[64,128,128,1,1]{2,0,1,4,3:T(8,128)(2,1)S(1)} %bitcast.151) | data formatting | bytes 4194304 | tf_op jit(solution)/shard_map/reshape | solution.py:92
  63.4 3.7 %reshape.385 = bf16[2,768,768]{2,1,0:T(8,128)(2,1)} reshape(bf16[2,6,128,6,128]{4,3,2,1,0:T(8,128)(2,1)S(1)} %copy.63) | data formatting | bytes 4718592 | tf_op jit(solution)/shard_map/reshape | solution.py:114
  67.1 3.5 %fusion.6 = f32[2,512,768]{2,1,0:T(8,128)S(1)} fusion(bf16[2,768,768]{2,1,0:T(8,128)(2,1)} %reshape.385, bf16[2,256,768]{2,1,0:T(8,128)(2,1)} %subtract_convert_fusion.3, bf16[2,256,768]{2,1,0:T(8,128)(2,1)} %fusion.31), kind=kOutput, calls=%fused_computation.13 | convolution fusion | flops 1211105280 | bytes 7077888 | tf_op jit(solution)/shard_map/ncm,nmk->nck/dot_general | solution.py:134
  70.9 4.6 %collective-permute-start.2 = (f32[256,256]{1,0:T(8,128)S(1)}, f32[256,256]{1,0:T(8,128)S(1)}, u32[]{:S(2)}, u32[]{:S(2)}) collective-permute-start(f32[256,256]{1,0:T(8,128)S(1)} %get-tuple-element.27), channel_id=1, source_target_pairs={{4,0},{8,4},{12,8},{16,12},{20,16},{24,20},{28,24},{32,28},{36,32}... | collective-permute-start | bytes 786440 | tf_op jit(solution)/shard_map/ppermute | solution.py:17
  76.8 2.6 %collective-permute-done.2 = f32[256,256]{1,0:T(8,128)S(1)} collective-permute-done((f32[256,256]{1,0:T(8,128)S(1)}, f32[256,256]{1,0:T(8,128)S(1)}, u32[]{:S(2)}, u32[]{:S(2)}) %collective-permute-start.2) | collective-permute-done | bytes 262176 | tf_op jit(solution)/shard_map/ppermute | solution.py:17
  79.5 6.1 %collective-permute-done.3 = f32[2,256,128]{2,1,0:T(8,128)S(1)} collective-permute-done((f32[2,256,128]{2,1,0:T(8,128)S(1)}, f32[2,256,128]{2,1,0:T(8,128)S(1)}, u32[]{:S(2)}, u32[]{:S(2)}) %collective-permute-start.3) | collective-permute-done | bytes 262176 | tf_op jit(solution)/shard_map/ppermute | solution.py:17
  85.9 2.5 %collective-permute-start.4 = (f32[256,256]{1,0:T(8,128)S(1)}, f32[256,256]{1,0:T(8,128)S(1)}, u32[]{:S(2)}, u32[]{:S(2)}) collective-permute-start(f32[256,256]{1,0:T(8,128)S(1)} %get-tuple-element.32), channel_id=1, source_target_pairs={{0,4},{4,8},{8,12},{12,16},{16,20},{20,24},{24,28},{28,32},{32,36}... | collective-permute-start | bytes 786440 | tf_op jit(solution)/shard_map/ppermute | solution.py:17
  88.4 3.6 %collective-permute-start.5 = (f32[2,256,128]{2,1,0:T(8,128)S(1)}, f32[2,256,128]{2,1,0:T(8,128)S(1)}, u32[]{:S(2)}, u32[]{:S(2)}) collective-permute-start(f32[2,256,128]{2,1,0:T(8,128)S(1)} %slice.230), channel_id=1, source_target_pairs={{0,1},{1,2},{2,3},{4,5},{5,6},{6,7},{8,9},{9,10},{10,11},{12,13},{... | collective-permute-start | bytes 786440 | tf_op jit(solution)/shard_map/ppermute | solution.py:17
  92.1 5.4 %collective-permute-done.5 = f32[2,256,128]{2,1,0:T(8,128)S(1)} collective-permute-done((f32[2,256,128]{2,1,0:T(8,128)S(1)}, f32[2,256,128]{2,1,0:T(8,128)S(1)}, u32[]{:S(2)}, u32[]{:S(2)}) %collective-permute-start.5) | collective-permute-done | bytes 262176 | tf_op jit(solution)/shard_map/ppermute | solution.py:17
  100.9 2.9 %collective-permute-start.6 = (f32[256,256]{1,0:T(8,128)S(1)}, f32[256,256]{1,0:T(8,128)S(1)}, u32[]{:S(2)}, u32[]{:S(2)}) collective-permute-start(f32[256,256]{1,0:T(8,128)S(1)} %get-tuple-element.25), channel_id=1, source_target_pairs={{4,0},{8,4},{12,8},{16,12},{20,16},{24,20},{28,24},{32,28},{36,32}... | collective-permute-start | bytes 786440 | tf_op jit(solution)/shard_map/ppermute | solution.py:17
  105.1 3.5 %collective-permute-done.6 = f32[256,256]{1,0:T(8,128)S(1)} collective-permute-done((f32[256,256]{1,0:T(8,128)S(1)}, f32[256,256]{1,0:T(8,128)S(1)}, u32[]{:S(2)}, u32[]{:S(2)}) %collective-permute-start.6) | collective-permute-done | bytes 262176 | tf_op jit(solution)/shard_map/ppermute | solution.py:17
  108.6 3.0 %collective-permute-done.7 = f32[2,256,128]{2,1,0:T(8,128)S(1)} collective-permute-done((f32[2,256,128]{2,1,0:T(8,128)S(1)}, f32[2,256,128]{2,1,0:T(8,128)S(1)}, u32[]{:S(2)}, u32[]{:S(2)}) %collective-permute-start.7) | collective-permute-done | bytes 262176 | tf_op jit(solution)/shard_map/ppermute | solution.py:17
  111.9 5.9 %collective-permute-start.8 = (f32[256,256]{1,0:T(8,128)S(1)}, f32[256,256]{1,0:T(8,128)S(1)}, u32[]{:S(2)}, u32[]{:S(2)}) collective-permute-start(f32[256,256]{1,0:T(8,128)S(1)} %get-tuple-element.30), channel_id=1, source_target_pairs={{0,4},{4,8},{8,12},{12,16},{16,20},{20,24},{24,28},{28,32},{32,36}... | collective-permute-start | bytes 786440 | tf_op jit(solution)/shard_map/ppermute | solution.py:17
  117.8 3.4 %collective-permute-start.9 = (f32[2,256,128]{2,1,0:T(8,128)S(1)}, f32[2,256,128]{2,1,0:T(8,128)S(1)}, u32[]{:S(2)}, u32[]{:S(2)}) collective-permute-start(f32[2,256,128]{2,1,0:T(8,128)S(1)} %slice.241), channel_id=1, source_target_pairs={{0,1},{1,2},{2,3},{4,5},{5,6},{6,7},{8,9},{9,10},{10,11},{12,13},{... | collective-permute-start | bytes 786440 | tf_op jit(solution)/shard_map/ppermute | solution.py:17
  121.3 5.5 %collective-permute-done.9 = f32[2,256,128]{2,1,0:T(8,128)S(1)} collective-permute-done((f32[2,256,128]{2,1,0:T(8,128)S(1)}, f32[2,256,128]{2,1,0:T(8,128)S(1)}, u32[]{:S(2)}, u32[]{:S(2)}) %collective-permute-start.9) | collective-permute-done | bytes 262176 | tf_op jit(solution)/shard_map/ppermute | solution.py:17
  128.7 2.8 %collective-permute-start.10 = (f32[256,256]{1,0:T(8,128)S(1)}, f32[256,256]{1,0:T(8,128)S(1)}, u32[]{:S(2)}, u32[]{:S(2)}) collective-permute-start(f32[256,256]{1,0:T(8,128)S(1)} %get-tuple-element.23), channel_id=1, source_target_pairs={{4,0},{8,4},{12,8},{16,12},{20,16},{24,20},{28,24},{32,28},{36,32}... | collective-permute-start | bytes 786440 | tf_op jit(solution)/shard_map/ppermute | solution.py:17
  133.0 3.3 %collective-permute-done.10 = f32[256,256]{1,0:T(8,128)S(1)} collective-permute-done((f32[256,256]{1,0:T(8,128)S(1)}, f32[256,256]{1,0:T(8,128)S(1)}, u32[]{:S(2)}, u32[]{:S(2)}) %collective-permute-start.10) | collective-permute-done | bytes 262176 | tf_op jit(solution)/shard_map/ppermute | solution.py:17
  136.4 3.4 %collective-permute-done.11 = f32[2,256,128]{2,1,0:T(8,128)S(1)} collective-permute-done((f32[2,256,128]{2,1,0:T(8,128)S(1)}, f32[2,256,128]{2,1,0:T(8,128)S(1)}, u32[]{:S(2)}, u32[]{:S(2)}) %collective-permute-start.11) | collective-permute-done | bytes 262176 | tf_op jit(solution)/shard_map/ppermute | solution.py:17
  140.2 4.7 %collective-permute-start.12 = (f32[256,256]{1,0:T(8,128)S(1)}, f32[256,256]{1,0:T(8,128)S(1)}, u32[]{:S(2)}, u32[]{:S(2)}) collective-permute-start(f32[256,256]{1,0:T(8,128)S(1)} %get-tuple-element.28), channel_id=1, source_target_pairs={{0,4},{4,8},{8,12},{12,16},{16,20},{20,24},{24,28},{28,32},{32,36}... | collective-permute-start | bytes 786440 | tf_op jit(solution)/shard_map/ppermute | solution.py:17
  144.9 3.4 %collective-permute-start.13 = (f32[2,256,128]{2,1,0:T(8,128)S(1)}, f32[2,256,128]{2,1,0:T(8,128)S(1)}, u32[]{:S(2)}, u32[]{:S(2)}) collective-permute-start(f32[2,256,128]{2,1,0:T(8,128)S(1)} %slice.252), channel_id=1, source_target_pairs={{0,1},{1,2},{2,3},{4,5},{5,6},{6,7},{8,9},{9,10},{10,11},{12,13},{... | collective-permute-start | bytes 786440 | tf_op jit(solution)/shard_map/ppermute | solution.py:17
  148.5 5.2 %collective-permute-done.13 = f32[2,256,128]{2,1,0:T(8,128)S(1)} collective-permute-done((f32[2,256,128]{2,1,0:T(8,128)S(1)}, f32[2,256,128]{2,1,0:T(8,128)S(1)}, u32[]{:S(2)}, u32[]{:S(2)}) %collective-permute-start.13) | collective-permute-done | bytes 262176 | tf_op jit(solution)/shard_map/ppermute | solution.py:17
  155.5 3.0 %collective-permute-start.14 = (f32[256,256]{1,0:T(8,128)S(1)}, f32[256,256]{1,0:T(8,128)S(1)}, u32[]{:S(2)}, u32[]{:S(2)}) collective-permute-start(f32[256,256]{1,0:T(8,128)S(1)} %get-tuple-element.21), channel_id=1, source_target_pairs={{4,0},{8,4},{12,8},{16,12},{20,16},{24,20},{28,24},{32,28},{36,32}... | collective-permute-start | bytes 786440 | tf_op jit(solution)/shard_map/ppermute | solution.py:17
  160.1 3.2 %collective-permute-done.14 = f32[256,256]{1,0:T(8,128)S(1)} collective-permute-done((f32[256,256]{1,0:T(8,128)S(1)}, f32[256,256]{1,0:T(8,128)S(1)}, u32[]{:S(2)}, u32[]{:S(2)}) %collective-permute-start.14) | collective-permute-done | bytes 262176 | tf_op jit(solution)/shard_map/ppermute | solution.py:17
  163.3 3.8 %collective-permute-done.15 = f32[2,256,128]{2,1,0:T(8,128)S(1)} collective-permute-done((f32[2,256,128]{2,1,0:T(8,128)S(1)}, f32[2,256,128]{2,1,0:T(8,128)S(1)}, u32[]{:S(2)}, u32[]{:S(2)}) %collective-permute-start.15) | collective-permute-done | bytes 262176 | tf_op jit(solution)/shard_map/ppermute | solution.py:17
  (115 shorter events, 26.1 us)
Async XLA Ops:
  2.6 8.8 %copy-start.6 = (s32[26,1]{0,1:T(1,128)S(1)}, s32[26,1]{0,1:T(1,128)}, u32[]{:S(2)}) copy-start(s32[26,1]{0,1:T(1,128)} %param.6) | copy-start | bytes 316
  15.9 7.9 %copy-start.4 = (s32[64,1]{0,1:T(1,128)S(1)}, s32[64,1]{0,1:T(1,128)}, u32[]{:S(2)}) copy-start(s32[64,1]{0,1:T(1,128)} %param.5) | copy-start | bytes 772
  15.9 8.6 %copy-start = (f32[2,1,256,384]{3,2,1,0:T(8,128)S(1)}, f32[2,1,256,384]{3,2,1,0:T(8,128)}, u32[]{:S(2)}) copy-start(f32[2,1,256,384]{3,2,1,0:T(8,128)} %param.8) | copy-start | bytes 2359300
  15.9 36.7 %all-to-all-start = ((bf16[32,2,128,128]{3,1,2,0:T(2,128)(2,1)}), bf16[32,2,128,128]{3,1,2,0:T(2,128)(2,1)}, u32[]{:S(2)}, u32[]{:S(2)}) async-start(bf16[32,2,128,128]{3,1,2,0:T(2,128)(2,1)} %copy.50), calls=%async_computation | async-start | bytes 4194304 | tf_op jit(solution)/shard_map/all_to_all | solution.py:91
  24.6 7.9 %copy-start.5 = (s32[6]{0:T(128)S(1)}, s32[6]{0:T(128)}, u32[]{:S(2)}) copy-start(s32[6]{0:T(128)} %constant.126.clone) | copy-start | bytes 76
  24.7 25.9 %collective-permute-start = (f32[256,256]{1,0:T(8,128)S(1)}, f32[256,256]{1,0:T(8,128)S(1)}, u32[]{:S(2)}, u32[]{:S(2)}) collective-permute-start(f32[256,256]{1,0:T(8,128)S(1)} %get-tuple-element.34), channel_id=1, source_target_pairs={{0,4},{4,8},{8,12},{12,16},{16,20},{20,24},{24,28},{28,32},{32,36}... | collective-permute-start | bytes 786440 | tf_op jit(solution)/shard_map/ppermute | solution.py:17
  28.1 9.2 %collective-permute-start.1 = (f32[2,256,128]{2,1,0:T(8,128)S(1)}, f32[2,256,128]{2,1,0:T(8,128)S(1)}, u32[]{:S(2)}, u32[]{:S(2)}) collective-permute-start(f32[2,256,128]{2,1,0:T(8,128)S(1)} %slice.219), channel_id=1, source_target_pairs={{0,1},{1,2},{2,3},{4,5},{5,6},{6,7},{8,9},{9,10},{10,11},{12,13},{... | collective-permute-start | bytes 786440 | tf_op jit(solution)/shard_map/ppermute | solution.py:17
  60.0 1.6 copy-start.2
  70.8 14.8 %copy-start.1 = (f32[2,1,256,384]{3,2,1,0:T(8,128)S(1)}, f32[2,1,256,384]{3,2,1,0:T(8,128)}, u32[]{:S(2)}) copy-start(f32[2,1,256,384]{3,2,1,0:T(8,128)} %param.8) | copy-start | bytes 2359300
  70.9 8.6 %collective-permute-start.2 = (f32[256,256]{1,0:T(8,128)S(1)}, f32[256,256]{1,0:T(8,128)S(1)}, u32[]{:S(2)}, u32[]{:S(2)}) collective-permute-start(f32[256,256]{1,0:T(8,128)S(1)} %get-tuple-element.27), channel_id=1, source_target_pairs={{4,0},{8,4},{12,8},{16,12},{20,16},{24,20},{28,24},{32,28},{36,32}... | collective-permute-start | bytes 786440 | tf_op jit(solution)/shard_map/ppermute | solution.py:17
  75.5 10.1 %collective-permute-start.3 = (f32[2,256,128]{2,1,0:T(8,128)S(1)}, f32[2,256,128]{2,1,0:T(8,128)S(1)}, u32[]{:S(2)}, u32[]{:S(2)}) collective-permute-start(f32[2,256,128]{2,1,0:T(8,128)S(1)} %slice.226), channel_id=1, source_target_pairs={{1,0},{2,1},{3,2},{5,4},{6,5},{7,6},{9,8},{10,9},{11,10},{13,12},{... | collective-permute-start | bytes 786440 | tf_op jit(solution)/shard_map/ppermute | solution.py:17
  85.9 6.1 %collective-permute-start.4 = (f32[256,256]{1,0:T(8,128)S(1)}, f32[256,256]{1,0:T(8,128)S(1)}, u32[]{:S(2)}, u32[]{:S(2)}) collective-permute-start(f32[256,256]{1,0:T(8,128)S(1)} %get-tuple-element.32), channel_id=1, source_target_pairs={{0,4},{4,8},{8,12},{12,16},{16,20},{20,24},{24,28},{28,32},{32,36}... | collective-permute-start | bytes 786440 | tf_op jit(solution)/shard_map/ppermute | solution.py:17
  88.4 9.1 %collective-permute-start.5 = (f32[2,256,128]{2,1,0:T(8,128)S(1)}, f32[2,256,128]{2,1,0:T(8,128)S(1)}, u32[]{:S(2)}, u32[]{:S(2)}) collective-permute-start(f32[2,256,128]{2,1,0:T(8,128)S(1)} %slice.230), channel_id=1, source_target_pairs={{0,1},{1,2},{2,3},{4,5},{5,6},{6,7},{8,9},{9,10},{10,11},{12,13},{... | collective-permute-start | bytes 786440 | tf_op jit(solution)/shard_map/ppermute | solution.py:17
  97.6 1.7 copy-start.3
  100.9 7.7 %collective-permute-start.6 = (f32[256,256]{1,0:T(8,128)S(1)}, f32[256,256]{1,0:T(8,128)S(1)}, u32[]{:S(2)}, u32[]{:S(2)}) collective-permute-start(f32[256,256]{1,0:T(8,128)S(1)} %get-tuple-element.25), channel_id=1, source_target_pairs={{4,0},{8,4},{12,8},{16,12},{20,16},{24,20},{28,24},{32,28},{36,32}... | collective-permute-start | bytes 786440 | tf_op jit(solution)/shard_map/ppermute | solution.py:17
  103.8 7.9 %collective-permute-start.7 = (f32[2,256,128]{2,1,0:T(8,128)S(1)}, f32[2,256,128]{2,1,0:T(8,128)S(1)}, u32[]{:S(2)}, u32[]{:S(2)}) collective-permute-start(f32[2,256,128]{2,1,0:T(8,128)S(1)} %slice.237), channel_id=1, source_target_pairs={{1,0},{2,1},{3,2},{5,4},{6,5},{7,6},{9,8},{10,9},{11,10},{13,12},{... | collective-permute-start | bytes 786440 | tf_op jit(solution)/shard_map/ppermute | solution.py:17
  111.9 9.3 %collective-permute-start.8 = (f32[256,256]{1,0:T(8,128)S(1)}, f32[256,256]{1,0:T(8,128)S(1)}, u32[]{:S(2)}, u32[]{:S(2)}) collective-permute-start(f32[256,256]{1,0:T(8,128)S(1)} %get-tuple-element.30), channel_id=1, source_target_pairs={{0,4},{4,8},{8,12},{12,16},{16,20},{20,24},{24,28},{28,32},{32,36}... | collective-permute-start | bytes 786440 | tf_op jit(solution)/shard_map/ppermute | solution.py:17
  117.8 9.0 %collective-permute-start.9 = (f32[2,256,128]{2,1,0:T(8,128)S(1)}, f32[2,256,128]{2,1,0:T(8,128)S(1)}, u32[]{:S(2)}, u32[]{:S(2)}) collective-permute-start(f32[2,256,128]{2,1,0:T(8,128)S(1)} %slice.241), channel_id=1, source_target_pairs={{0,1},{1,2},{2,3},{4,5},{5,6},{6,7},{8,9},{9,10},{10,11},{12,13},{... | collective-permute-start | bytes 786440 | tf_op jit(solution)/shard_map/ppermute | solution.py:17
  128.7 7.7 %collective-permute-start.10 = (f32[256,256]{1,0:T(8,128)S(1)}, f32[256,256]{1,0:T(8,128)S(1)}, u32[]{:S(2)}, u32[]{:S(2)}) collective-permute-start(f32[256,256]{1,0:T(8,128)S(1)} %get-tuple-element.23), channel_id=1, source_target_pairs={{4,0},{8,4},{12,8},{16,12},{20,16},{24,20},{28,24},{32,28},{36,32}... | collective-permute-start | bytes 786440 | tf_op jit(solution)/shard_map/ppermute | solution.py:17
  131.5 8.4 %collective-permute-start.11 = (f32[2,256,128]{2,1,0:T(8,128)S(1)}, f32[2,256,128]{2,1,0:T(8,128)S(1)}, u32[]{:S(2)}, u32[]{:S(2)}) collective-permute-start(f32[2,256,128]{2,1,0:T(8,128)S(1)} %slice.248), channel_id=1, source_target_pairs={{1,0},{2,1},{3,2},{5,4},{6,5},{7,6},{9,8},{10,9},{11,10},{13,12},{... | collective-permute-start | bytes 786440 | tf_op jit(solution)/shard_map/ppermute | solution.py:17
  140.2 8.3 %collective-permute-start.12 = (f32[256,256]{1,0:T(8,128)S(1)}, f32[256,256]{1,0:T(8,128)S(1)}, u32[]{:S(2)}, u32[]{:S(2)}) collective-permute-start(f32[256,256]{1,0:T(8,128)S(1)} %get-tuple-element.28), channel_id=1, source_target_pairs={{0,4},{4,8},{8,12},{12,16},{16,20},{20,24},{24,28},{28,32},{32,36}... | collective-permute-start | bytes 786440 | tf_op jit(solution)/shard_map/ppermute | solution.py:17
  144.9 8.7 %collective-permute-start.13 = (f32[2,256,128]{2,1,0:T(8,128)S(1)}, f32[2,256,128]{2,1,0:T(8,128)S(1)}, u32[]{:S(2)}, u32[]{:S(2)}) collective-permute-start(f32[2,256,128]{2,1,0:T(8,128)S(1)} %slice.252), channel_id=1, source_target_pairs={{0,1},{1,2},{2,3},{4,5},{5,6},{6,7},{8,9},{9,10},{10,11},{12,13},{... | collective-permute-start | bytes 786440 | tf_op jit(solution)/shard_map/ppermute | solution.py:17
  155.5 7.7 %collective-permute-start.14 = (f32[256,256]{1,0:T(8,128)S(1)}, f32[256,256]{1,0:T(8,128)S(1)}, u32[]{:S(2)}, u32[]{:S(2)}) collective-permute-start(f32[256,256]{1,0:T(8,128)S(1)} %get-tuple-element.21), channel_id=1, source_target_pairs={{4,0},{8,4},{12,8},{16,12},{20,16},{24,20},{28,24},{32,28},{36,32}... | collective-permute-start | bytes 786440 | tf_op jit(solution)/shard_map/ppermute | solution.py:17
  158.7 8.4 %collective-permute-start.15 = (f32[2,256,128]{2,1,0:T(8,128)S(1)}, f32[2,256,128]{2,1,0:T(8,128)S(1)}, u32[]{:S(2)}, u32[]{:S(2)}) collective-permute-start(f32[2,256,128]{2,1,0:T(8,128)S(1)} %slice.259), channel_id=1, source_target_pairs={{1,0},{2,1},{3,2},{5,4},{6,5},{7,6},{9,8},{10,9},{11,10},{13,12},{... | collective-permute-start | bytes 786440 | tf_op jit(solution)/shard_map/ppermute | solution.py:17

commit v2 on v1

--- a/solution.py
+++ b/solution.py
@@ -87,7 +87,7 @@
     send_tiles = jnp.einsum(
         "mj,jab->mab", pick_send, tiles, preferred_element_type=jnp.float32
     ).astype(jnp.bfloat16)
-    send_tiles = send_tiles.reshape(gx_count, slot_cap, block_len, block_len)
+    send_tiles = send_tiles.reshape(gx_count, slot_cap * block_len, block_len)
     got_tiles = lax.all_to_all(send_tiles, "gx", split_axis=0, concat_axis=0, tiled=True)
     got_tiles = got_tiles.reshape(slot_count, block_len, block_len)
 
@@ -119,18 +119,21 @@
     cheb_radius = (CHEB_HIGH - CHEB_LOW) / 2.0
     cheb_ratio = cheb_center / cheb_radius
     cheb_rho = 1.0 / cheb_ratio
+    west_residual = from_behind(residual[sub_count - 1, :, : 2 * block_len], "gx", 1)
+    south_residual = from_behind(residual[..., 2 * block_len :], "gy", 1)
     update = residual / cheb_center
+    west_update = west_residual / cheb_center
+    south_update = south_residual / cheb_center
     multipliers = jnp.zeros_like(residual)
     for sweep in range(ITERS):
         multipliers = multipliers + update
         east_part = update[..., : 2 * block_len]
         to_north_part = update[..., 2 * block_len :]
-        from_west = from_behind(east_part[sub_count - 1], "gx", 1)
-        from_south = from_behind(to_north_part, "gy", 1)
-        west_in = -jnp.concatenate([from_west[None], east_part[: sub_count - 1]], axis=0)
-        local_vec = jnp.concatenate([west_in, east_part, -from_south, to_north_part], axis=-1)
-        high = local_vec.astype(jnp.bfloat16)
-        low = (local_vec - high.astype(jnp.float32)).astype(jnp.bfloat16)
+        west_in = -jnp.concatenate([west_update[None], east_part[: sub_count - 1]], axis=0)
+        local_vec = jnp.concatenate([west_in, east_part, -south_update, to_north_part], axis=-1)
+        high_f = lax.reduce_precision(local_vec, exponent_bits=8, mantissa_bits=7)
+        high = high_f.astype(jnp.bfloat16)
+        low = (local_vec - high_f).astype(jnp.bfloat16)
         both = jnp.einsum(
             "ncm,nmk->nck",
             jnp.concatenate([high, low], axis=1),
@@ -144,12 +147,23 @@
         split_north_part = image[..., 5 * block_len :]
         from_east = from_behind(west_part[0], "gx", -1)
         from_north = from_behind(south_part, "gy", -1)
+        last = sweep == ITERS - 1
+        if not last:
+            west_east_part = from_behind(split_east_part[sub_count - 1], "gx", 1)
+            south_north_part = from_behind(split_north_part, "gy", 1)
         east_near = jnp.concatenate([west_part[1:], from_east[None]], axis=0)
         residual = residual - jnp.concatenate(
             [split_east_part - east_near, split_north_part - from_north], axis=-1
         )
         rho_next = 1.0 / (2.0 * cheb_ratio - cheb_rho)
-        update = rho_next * cheb_rho * update + 2.0 * rho_next / cheb_radius * residual
+        keep = rho_next * cheb_rho
+        step = 2.0 * rho_next / cheb_radius
+        update = keep * update + step * residual
+        if not last:
+            west_residual = west_residual - (west_east_part - west_part[0])
+            south_residual = south_residual - (south_north_part - south_part)
+            west_update = keep * west_update + step * west_residual
+            south_update = keep * south_update + step * south_residual
         cheb_rho = rho_next
     return (multipliers[:, None], residual[:, None])
 

time: 172 us -> 144 us (0.84); the launches traced: 169 us -> 143 us
  waiting for transfers between devices: 62.8 us -> 30.3 us
  starting transfers between devices: 57.1 us -> 61.7 us
  other arithmetic: 9.33 us -> 11.6 us
    ppermute x16, waiting for transfers between devices: 62.8 us -> 30.3 us  [from_behind(): lax.ppermute(value, axis, [(source, source + steps) for source in range(i...]
    ppermute x16, starting transfers between devices: 49.2 us -> 53.8 us  [from_behind(): lax.ppermute(value, axis, [(source, source + steps) for source in range(i...]
    all_to_all x1 -> x0, local copies, waits for them, and re-layouts: 3.95 us -> none  [shards(): lax.all_to_all(send_tiles, 'gx', split_axis=0, concat_axis=0, tiled=True)]
    reshape x1 -> x0, local copies, waits for them, and re-layouts: 3.52 us -> none  [shards(): send_tiles = send_tiles.reshape(gx_count, slot_cap, block_len, block_len)]
    convert_element_type x0 -> x1, local copies, waits for them, and re-layouts: none -> 2.71 us  [shards(): send_tiles = jnp.einsum('mj,jab->mab', pick_send, tiles, preferred_elemen...]
    unnamed x14, local copies, waits for them, and re-layouts: 2.14 us -> 0.03 us
    div x1, other arithmetic: 0.07 us -> 2.13 us  [shards(): update = residual / cheb_center]
    slice x0 -> x8, local copies, waits for them, and re-layouts: none -> 1.85 us  [the longest x4 1.03 us: shards(): east_part[:sub_count - 1]]
  transfers between devices with their start and end apart: 17 -> 17, of which waited for: 13 -> 9; matrix products, arithmetic and copies ran while one was open for 3% -> 8% of each run, Pallas kernels for 0% -> 0%
where the time goes in v2:
time: 144 us; the launch traced here: 143 us
  starting transfers between devices  61.7 us (43%)
  waiting for transfers between devices  30.3 us (21%)
  matrix products  19.2 us (13%)
  local copies, waits for them, and re-layouts  18.9 us (13%)
  other arithmetic  11.6 us (8%)
    ppermute x16, starting transfers between devices, from_behind(): lax.ppermute(value, axis, [(source, source + steps) for source in range(i...  53.8 us
    ppermute x16, waiting for transfers between devices, from_behind(): lax.ppermute(value, axis, [(source, source + steps) for source in range(i...  30.3 us
    dot_general x1, matrix products, shards(): jnp.einsum('jka,jkb->jab', factor_panels[:, 0, 0], factor_panels[:, 0, 1]...  8.61 us
    all_to_all x1, starting transfers between devices, shards(): lax.all_to_all(send_tiles, 'gx', split_axis=0, concat_axis=0, tiled=True)  7.84 us
    dot_general x4, matrix products, shards(): jnp.einsum('ncm,nmk->nck', jnp.concatenate([high, low], axis=1), matrices...  6.95 us
    reshape x1, local copies, waits for them, and re-layouts, shards(): matrices.astype(jnp.bfloat16)  5 us
    reshape x1, local copies, waits for them, and re-layouts, shards(): got_tiles = got_tiles.reshape(slot_count, block_len, block_len)  2.9 us
  transfers between devices with their start and end apart: 17, of which 9 were waited for; matrix products, arithmetic and copies ran while one was open for 8% of the time, Pallas kernels for 0%

profile of v2, /device:TPU:17, one launch (start us, length us, event | category | flops | bytes accessed | tf_op | source)
XLA Modules:
  0.0 143.0 jit_solution(5726393455616583747)
XLA Ops:
  2.7 8.6 %fusion.28 = bf16[26,128,128]{2,1,0:T(8,128)(2,1)S(1)} fusion(bf16[26,1,2,1536,128]{4,3,2,1,0:T(8,128)(2,1)} %param.7), kind=kOutput, calls=%fused_computation.46 | convolution fusion | flops 1309048832 | bytes 21299200 | tf_op jit(solution)/shard_map/jka,jkb->jab/dot_general | solution.py:64
  12.4 2.7 %copy.53 = bf16[64,128,128]{2,1,0:T(8,128)(2,1)} copy(bf16[64,128,128]{2,0,1:T(8,128)(2,1)S(1)} %convolution_convert_fusion) | data formatting | bytes 4194304 | tf_op jit(solution)/shard_map/convert_element_type | solution.py:89
  15.1 7.8 %all-to-all-start = ((bf16[32,256,128]{2,1,0:T(8,128)(2,1)}), bf16[32,256,128]{2,1,0:T(8,128)(2,1)S(1)}, u32[]{:S(2)}, u32[]{:S(2)}) async-start(bf16[32,256,128]{2,1,0:T(8,128)(2,1)} %bitcast.154), calls=%async_computation | async-start | bytes 4194304 | tf_op jit(solution)/shard_map/all_to_all | solution.py:91
  23.7 2.1 %broadcast_multiply_fusion = (f32[2,256,384]{2,1,0:T(8,128)}, f32[2,256,384]{2,1,0:T(8,128)S(1)}) fusion(f32[2,384]{1,0:T(2,128)S(1)} %pad_convert_fusion, f32[2,1,256,384]{3,2,1,0:T(8,128)} %param.8), kind=kLoop, calls=%fused_computation.72 | loop fusion | flops 393216 | bytes 2362368 | tf_op jit(solution)/shard_map/div | solution.py:124
  26.5 3.4 %collective-permute-start = (f32[256,256]{1,0:T(8,128)}, f32[256,256]{1,0:T(8,128)S(1)}, u32[]{:S(2)}, u32[]{:S(2)}) collective-permute-start(f32[256,256]{1,0:T(8,128)} %slice_bitcast_fusion.7), channel_id=1, source_target_pairs={{0,4},{4,8},{8,12},{12,16},{16,20},{20,24},{24,28},{28,32},{32,36}... | collective-permute-start | bytes 786440 | tf_op jit(solution)/shard_map/ppermute | solution.py:17
  30.6 3.5 %collective-permute-start.1 = (f32[2,256,128]{2,1,0:T(8,128)}, f32[2,256,128]{2,1,0:T(8,128)S(1)}, u32[]{:S(2)}, u32[]{:S(2)}) collective-permute-start(f32[2,256,128]{2,1,0:T(8,128)} %slice.225), channel_id=1, source_target_pairs={{0,1},{1,2},{2,3},{4,5},{5,6},{6,7},{8,9},{9,10},{10,11},{12,13},{... | collective-permute-start | bytes 786440 | tf_op jit(solution)/shard_map/ppermute | solution.py:17
  38.2 11.7 %collective-permute-done = f32[256,256]{1,0:T(8,128)S(1)} collective-permute-done((f32[256,256]{1,0:T(8,128)}, f32[256,256]{1,0:T(8,128)S(1)}, u32[]{:S(2)}, u32[]{:S(2)}) %collective-permute-start) | collective-permute-done | bytes 262176 | tf_op jit(solution)/shard_map/ppermute | solution.py:17
  50.0 1.5 %reduce-precision_convert_fusion.3 = (bf16[2,256,768]{2,1,0:T(8,128)(2,1)}, bf16[2,256,768]{2,1,0:T(8,128)(2,1)}) fusion(f32[2,256,128]{2,1,0:T(8,128)S(1)} %slice.226, f32[2,256,128]{2,1,0:T(8,128)S(1)} %multiply_negate_fusion, f32[2,256,256]{2,1,0:T(8,128)S(1)} %slice.224, f32[2,256,256]{2,1,0:T(8,128)S(1)} %maximum_negate_fusion), kind=kLoop, calls=%fused_computation.14 | loop fusion | flops 2752512 | bytes 3145728 | tf_op jit(solution)/shard_map/convert_element_type | solution.py:135
  51.5 2.9 %copy.70 = bf16[64,128,128,1,1]{1,0,4,3,2:T(8,128)(2,1)} copy(bf16[64,128,128,1,1]{2,1,0,4,3:T(8,128)(2,1)S(1)} %bitcast.152) | data formatting | bytes 4194304 | tf_op jit(solution)/shard_map/reshape | solution.py:92
  54.4 1.7 %fusion.6 = f32[128,128,2,6,6]{1,4,3,2,0:T(8,128)S(1)} fusion(bf16[64,128,128,1,1]{2,1,0,4,3:T(8,128)(2,1)S(1)} %bitcast.153, s32[2,6,6]{2,1,0:T(8,128)S(1)} %fusion.60, pred[2,6,6]{2,1,0:T(8,128)(4,1)S(1)} %get-tuple-element.56), kind=kOutput, calls=%fused_computation.15 | convolution fusion | flops 151004160 | bytes 6816104 | tf_op jit(solution)/shard_map/spqf,fab->spaqb/dot_general | solution.py:109
  57.2 2.4 %copy.66 = bf16[2,6,128,6,128]{4,3,2,1,0:T(8,128)(2,1)} copy(bf16[2,6,128,6,128]{4,3,1,0,2:T(8,128)(2,1)S(1)} %fusion.5) | data formatting | bytes 4718592 | tf_op jit(solution)/shard_map/convert_element_type | solution.py:114
  59.5 5.0 %reshape.385 = bf16[2,768,768]{2,1,0:T(8,128)(2,1)S(1)} reshape(bf16[2,6,128,6,128]{4,3,2,1,0:T(8,128)(2,1)} %copy.66) | data formatting | bytes 4718592 | tf_op jit(solution)/shard_map/reshape | solution.py:114
  64.5 2.8 %fusion.12 = f32[2,512,768]{2,1,0:T(8,128)S(1)} fusion(bf16[2,768,768]{2,1,0:T(8,128)(2,1)S(1)} %reshape.385, bf16[2,256,768]{2,1,0:T(8,128)(2,1)} %get-tuple-element.54, bf16[2,256,768]{2,1,0:T(8,128)(2,1)} %get-tuple-element.53), kind=kOutput, calls=%fused_computation.27 | convolution fusion | flops 1211105280 | bytes 7077888 | tf_op jit(solution)/shard_map/ncm,nmk->nck/dot_general | solution.py:137
  67.6 4.5 %collective-permute-start.2 = (f32[256,256]{1,0:T(8,128)S(1)}, f32[256,256]{1,0:T(8,128)S(1)}, u32[]{:S(2)}, u32[]{:S(2)}) collective-permute-start(f32[256,256]{1,0:T(8,128)S(1)} %get-tuple-element.48), channel_id=1, source_target_pairs={{4,0},{8,4},{12,8},{16,12},{20,16},{24,20},{28,24},{32,28},{36,32}... | collective-permute-start | bytes 786440 | tf_op jit(solution)/shard_map/ppermute | solution.py:17
  73.5 4.2 %collective-permute-start.5 = (f32[2,256,128]{2,1,0:T(8,128)S(1)}, f32[2,256,128]{2,1,0:T(8,128)S(1)}, u32[]{:S(2)}, u32[]{:S(2)}) collective-permute-start(f32[2,256,128]{2,1,0:T(8,128)S(1)} %get-tuple-element.51), channel_id=1, source_target_pairs={{0,1},{1,2},{2,3},{4,5},{5,6},{6,7},{8,9},{9,10},{10,11},{12,13},{... | collective-permute-start | bytes 786440 | tf_op jit(solution)/shard_map/ppermute | solution.py:17
  77.6 2.4 %collective-permute-start.4 = (f32[256,256]{1,0:T(8,128)S(1)}, f32[256,256]{1,0:T(8,128)S(1)}, u32[]{:S(2)}, u32[]{:S(2)}) collective-permute-start(f32[256,256]{1,0:T(8,128)S(1)} %get-tuple-element.47), channel_id=1, source_target_pairs={{0,4},{4,8},{8,12},{12,16},{16,20},{20,24},{24,28},{28,32},{32,36}... | collective-permute-start | bytes 786440 | tf_op jit(solution)/shard_map/ppermute | solution.py:17
  80.1 2.1 %collective-permute-done.3 = f32[2,256,128]{2,1,0:T(8,128)S(1)} collective-permute-done((f32[2,256,128]{2,1,0:T(8,128)S(1)}, f32[2,256,128]{2,1,0:T(8,128)S(1)}, u32[]{:S(2)}, u32[]{:S(2)}) %collective-permute-start.3) | collective-permute-done | bytes 262176 | tf_op jit(solution)/shard_map/ppermute | solution.py:17
  83.9 1.4 fusion.16
  85.5 6.2 %collective-permute-start.6 = (f32[256,256]{1,0:T(8,128)S(1)}, f32[256,256]{1,0:T(8,128)S(1)}, u32[]{:S(2)}, u32[]{:S(2)}) collective-permute-start(f32[256,256]{1,0:T(8,128)S(1)} %get-tuple-element.40), channel_id=1, source_target_pairs={{4,0},{8,4},{12,8},{16,12},{20,16},{24,20},{28,24},{32,28},{36,32}... | collective-permute-start | bytes 786440 | tf_op jit(solution)/shard_map/ppermute | solution.py:17
  93.1 4.2 %collective-permute-start.9 = (f32[2,256,128]{2,1,0:T(8,128)S(1)}, f32[2,256,128]{2,1,0:T(8,128)S(1)}, u32[]{:S(2)}, u32[]{:S(2)}) collective-permute-start(f32[2,256,128]{2,1,0:T(8,128)S(1)} %get-tuple-element.43), channel_id=1, source_target_pairs={{0,1},{1,2},{2,3},{4,5},{5,6},{6,7},{8,9},{9,10},{10,11},{12,13},{... | collective-permute-start | bytes 786440 | tf_op jit(solution)/shard_map/ppermute | solution.py:17
  97.3 1.9 %collective-permute-start.8 = (f32[256,256]{1,0:T(8,128)S(1)}, f32[256,256]{1,0:T(8,128)S(1)}, u32[]{:S(2)}, u32[]{:S(2)}) collective-permute-start(f32[256,256]{1,0:T(8,128)S(1)} %get-tuple-element.39), channel_id=1, source_target_pairs={{0,4},{4,8},{8,12},{12,16},{16,20},{20,24},{24,28},{28,32},{32,36}... | collective-permute-start | bytes 786440 | tf_op jit(solution)/shard_map/ppermute | solution.py:17
  99.3 2.6 %collective-permute-done.7 = f32[2,256,128]{2,1,0:T(8,128)S(1)} collective-permute-done((f32[2,256,128]{2,1,0:T(8,128)S(1)}, f32[2,256,128]{2,1,0:T(8,128)S(1)}, u32[]{:S(2)}, u32[]{:S(2)}) %collective-permute-start.7) | collective-permute-done | bytes 262176 | tf_op jit(solution)/shard_map/ppermute | solution.py:17
  103.7 1.4 fusion.20
  105.3 6.1 %collective-permute-start.10 = (f32[256,256]{1,0:T(8,128)S(1)}, f32[256,256]{1,0:T(8,128)S(1)}, u32[]{:S(2)}, u32[]{:S(2)}) collective-permute-start(f32[256,256]{1,0:T(8,128)S(1)} %get-tuple-element.31), channel_id=1, source_target_pairs={{4,0},{8,4},{12,8},{16,12},{20,16},{24,20},{28,24},{32,28},{36,32}... | collective-permute-start | bytes 786440 | tf_op jit(solution)/shard_map/ppermute | solution.py:17
  112.8 4.2 %collective-permute-start.13 = (f32[2,256,128]{2,1,0:T(8,128)S(1)}, f32[2,256,128]{2,1,0:T(8,128)S(1)}, u32[]{:S(2)}, u32[]{:S(2)}) collective-permute-start(f32[2,256,128]{2,1,0:T(8,128)S(1)} %get-tuple-element.35), channel_id=1, source_target_pairs={{0,1},{1,2},{2,3},{4,5},{5,6},{6,7},{8,9},{9,10},{10,11},{12,13},{... | collective-permute-start | bytes 786440 | tf_op jit(solution)/shard_map/ppermute | solution.py:17
  117.1 1.9 %collective-permute-start.12 = (f32[256,256]{1,0:T(8,128)S(1)}, f32[256,256]{1,0:T(8,128)S(1)}, u32[]{:S(2)}, u32[]{:S(2)}) collective-permute-start(f32[256,256]{1,0:T(8,128)S(1)} %get-tuple-element.30), channel_id=1, source_target_pairs={{0,4},{4,8},{8,12},{12,16},{16,20},{20,24},{24,28},{28,32},{32,36}... | collective-permute-start | bytes 786440 | tf_op jit(solution)/shard_map/ppermute | solution.py:17
  119.1 2.5 %collective-permute-done.11 = f32[2,256,128]{2,1,0:T(8,128)S(1)} collective-permute-done((f32[2,256,128]{2,1,0:T(8,128)S(1)}, f32[2,256,128]{2,1,0:T(8,128)S(1)}, u32[]{:S(2)}, u32[]{:S(2)}) %collective-permute-start.11) | collective-permute-done | bytes 262176 | tf_op jit(solution)/shard_map/ppermute | solution.py:17
  123.4 1.4 fusion.24
  125.1 6.1 %collective-permute-start.14 = (f32[256,256]{1,0:T(8,128)S(1)}, f32[256,256]{1,0:T(8,128)S(1)}, u32[]{:S(2)}, u32[]{:S(2)}) collective-permute-start(f32[256,256]{1,0:T(8,128)S(1)} %get-tuple-element.27), channel_id=1, source_target_pairs={{4,0},{8,4},{12,8},{16,12},{20,16},{24,20},{28,24},{32,28},{36,32}... | collective-permute-start | bytes 786440 | tf_op jit(solution)/shard_map/ppermute | solution.py:17
  131.3 1.3 collective-permute-start.15
  132.8 8.5 %collective-permute-done.15 = f32[2,256,128]{2,1,0:T(8,128)S(1)} collective-permute-done((f32[2,256,128]{2,1,0:T(8,128)S(1)}, f32[2,256,128]{2,1,0:T(8,128)S(1)}, u32[]{:S(2)}, u32[]{:S(2)}) %collective-permute-start.15) | collective-permute-done | bytes 262176 | tf_op jit(solution)/shard_map/ppermute | solution.py:17
  141.4 1.6 %fusion.36 = (f32[2,1,256,384]{3,2,1,0:T(8,128)}, f32[2,1,256,384]{3,2,1,0:T(8,128)}) fusion(f32[2,1,256,128]{3,2,0,1:T(8,128)S(1)} %fusion.38, f32[2,1,256,256]{3,2,0,1:T(8,128)S(1)} %fusion.37, f32[2,1,256,128]{3,2,0,1:T(8,128)S(1)} %bitcast.158, f32[2,1,256,256]{3,2,0,1:T(8,128)S(1)} %fusion.94, f32[2,1,256,128]{3,2,0,1:T(8,128)S(1)} %bitcast.157, ...), kind=kLoop, calls=%fused_computation.57 | loop fusion | flops 4325376 | bytes 5508096
  (113 shorter events, 20.9 us)
Async XLA Ops:
  2.6 8.8 %copy-start.6 = (s32[26,1]{0,1:T(1,128)S(1)}, s32[26,1]{0,1:T(1,128)}, u32[]{:S(2)}) copy-start(s32[26,1]{0,1:T(1,128)} %param.6) | copy-start | bytes 316
  15.1 7.9 %copy-start.4 = (s32[64,1]{0,1:T(1,128)S(1)}, s32[64,1]{0,1:T(1,128)}, u32[]{:S(2)}) copy-start(s32[64,1]{0,1:T(1,128)} %param.5) | copy-start | bytes 772
  15.1 36.4 %all-to-all-start = ((bf16[32,256,128]{2,1,0:T(8,128)(2,1)}), bf16[32,256,128]{2,1,0:T(8,128)(2,1)S(1)}, u32[]{:S(2)}, u32[]{:S(2)}) async-start(bf16[32,256,128]{2,1,0:T(8,128)(2,1)} %bitcast.154), calls=%async_computation | async-start | bytes 4194304 | tf_op jit(solution)/shard_map/all_to_all | solution.py:91
  23.7 11.1 %copy-start.5 = (s32[6]{0:T(128)S(1)}, s32[6]{0:T(128)}, u32[]{:S(2)}) copy-start(s32[6]{0:T(128)} %constant.144.clone) | copy-start | bytes 76
  26.5 23.4 %collective-permute-start = (f32[256,256]{1,0:T(8,128)}, f32[256,256]{1,0:T(8,128)S(1)}, u32[]{:S(2)}, u32[]{:S(2)}) collective-permute-start(f32[256,256]{1,0:T(8,128)} %slice_bitcast_fusion.7), channel_id=1, source_target_pairs={{0,4},{4,8},{8,12},{12,16},{16,20},{20,24},{24,28},{28,32},{32,36}... | collective-permute-start | bytes 786440 | tf_op jit(solution)/shard_map/ppermute | solution.py:17
  30.6 19.4 %collective-permute-start.1 = (f32[2,256,128]{2,1,0:T(8,128)}, f32[2,256,128]{2,1,0:T(8,128)S(1)}, u32[]{:S(2)}, u32[]{:S(2)}) collective-permute-start(f32[2,256,128]{2,1,0:T(8,128)} %slice.225), channel_id=1, source_target_pairs={{0,1},{1,2},{2,3},{4,5},{5,6},{6,7},{8,9},{9,10},{10,11},{12,13},{... | collective-permute-start | bytes 786440 | tf_op jit(solution)/shard_map/ppermute | solution.py:17
  50.0 1.5 %copy-start.2 = (f32[2,256,128]{2,1,0:T(8,128)}, f32[2,256,128]{2,1,0:T(8,128)S(1)}, u32[]{:S(2)}) copy-start(f32[2,256,128]{2,1,0:T(8,128)S(1)} %collective-permute-done.1) | copy-start | bytes 786436
  54.4 1.7 %copy-start = (bf16[64,128,128,1,1]{1,0,4,3,2:T(8,128)(2,1)S(1)}, bf16[64,128,128,1,1]{1,0,4,3,2:T(8,128)(2,1)}, u32[]{:S(2)}) copy-start(bf16[64,128,128,1,1]{1,0,4,3,2:T(8,128)(2,1)} %copy.70) | copy-start | bytes 6291460
  67.6 15.6 %copy-start.3 = (f32[2,256,128]{2,1,0:T(8,128)S(1)}, f32[2,256,128]{2,1,0:T(8,128)}, u32[]{:S(2)}) copy-start(f32[2,256,128]{2,1,0:T(8,128)} %copy-done.2) | copy-start | bytes 786436
  67.6 12.4 %collective-permute-start.2 = (f32[256,256]{1,0:T(8,128)S(1)}, f32[256,256]{1,0:T(8,128)S(1)}, u32[]{:S(2)}, u32[]{:S(2)}) collective-permute-start(f32[256,256]{1,0:T(8,128)S(1)} %get-tuple-element.48), channel_id=1, source_target_pairs={{4,0},{8,4},{12,8},{16,12},{20,16},{24,20},{28,24},{32,28},{36,32}... | collective-permute-start | bytes 786440 | tf_op jit(solution)/shard_map/ppermute | solution.py:17
  72.2 10.1 %collective-permute-start.3 = (f32[2,256,128]{2,1,0:T(8,128)S(1)}, f32[2,256,128]{2,1,0:T(8,128)S(1)}, u32[]{:S(2)}, u32[]{:S(2)}) collective-permute-start(f32[2,256,128]{2,1,0:T(8,128)S(1)} %get-tuple-element.52), channel_id=1, source_target_pairs={{1,0},{2,1},{3,2},{5,4},{6,5},{7,6},{9,8},{10,9},{11,10},{13,12},{... | collective-permute-start | bytes 786440 | tf_op jit(solution)/shard_map/ppermute | solution.py:17
  73.5 9.7 %collective-permute-start.5 = (f32[2,256,128]{2,1,0:T(8,128)S(1)}, f32[2,256,128]{2,1,0:T(8,128)S(1)}, u32[]{:S(2)}, u32[]{:S(2)}) collective-permute-start(f32[2,256,128]{2,1,0:T(8,128)S(1)} %get-tuple-element.51), channel_id=1, source_target_pairs={{0,1},{1,2},{2,3},{4,5},{5,6},{6,7},{8,9},{9,10},{10,11},{12,13},{... | collective-permute-start | bytes 786440 | tf_op jit(solution)/shard_map/ppermute | solution.py:17
  77.6 5.9 %collective-permute-start.4 = (f32[256,256]{1,0:T(8,128)S(1)}, f32[256,256]{1,0:T(8,128)S(1)}, u32[]{:S(2)}, u32[]{:S(2)}) collective-permute-start(f32[256,256]{1,0:T(8,128)S(1)} %get-tuple-element.47), channel_id=1, source_target_pairs={{0,4},{4,8},{8,12},{12,16},{16,20},{20,24},{24,28},{28,32},{32,36}... | collective-permute-start | bytes 786440 | tf_op jit(solution)/shard_map/ppermute | solution.py:17
  85.5 13.7 %collective-permute-start.6 = (f32[256,256]{1,0:T(8,128)S(1)}, f32[256,256]{1,0:T(8,128)S(1)}, u32[]{:S(2)}, u32[]{:S(2)}) collective-permute-start(f32[256,256]{1,0:T(8,128)S(1)} %get-tuple-element.40), channel_id=1, source_target_pairs={{4,0},{8,4},{12,8},{16,12},{20,16},{24,20},{28,24},{32,28},{36,32}... | collective-permute-start | bytes 786440 | tf_op jit(solution)/shard_map/ppermute | solution.py:17
  91.8 10.1 %collective-permute-start.7 = (f32[2,256,128]{2,1,0:T(8,128)S(1)}, f32[2,256,128]{2,1,0:T(8,128)S(1)}, u32[]{:S(2)}, u32[]{:S(2)}) collective-permute-start(f32[2,256,128]{2,1,0:T(8,128)S(1)} %get-tuple-element.44), channel_id=1, source_target_pairs={{1,0},{2,1},{3,2},{5,4},{6,5},{7,6},{9,8},{10,9},{11,10},{13,12},{... | collective-permute-start | bytes 786440 | tf_op jit(solution)/shard_map/ppermute | solution.py:17
  93.1 9.7 %collective-permute-start.9 = (f32[2,256,128]{2,1,0:T(8,128)S(1)}, f32[2,256,128]{2,1,0:T(8,128)S(1)}, u32[]{:S(2)}, u32[]{:S(2)}) collective-permute-start(f32[2,256,128]{2,1,0:T(8,128)S(1)} %get-tuple-element.43), channel_id=1, source_target_pairs={{0,1},{1,2},{2,3},{4,5},{5,6},{6,7},{8,9},{9,10},{10,11},{12,13},{... | collective-permute-start | bytes 786440 | tf_op jit(solution)/shard_map/ppermute | solution.py:17
  97.3 6.0 %collective-permute-start.8 = (f32[256,256]{1,0:T(8,128)S(1)}, f32[256,256]{1,0:T(8,128)S(1)}, u32[]{:S(2)}, u32[]{:S(2)}) collective-permute-start(f32[256,256]{1,0:T(8,128)S(1)} %get-tuple-element.39), channel_id=1, source_target_pairs={{0,4},{4,8},{8,12},{12,16},{16,20},{20,24},{24,28},{28,32},{32,36}... | collective-permute-start | bytes 786440 | tf_op jit(solution)/shard_map/ppermute | solution.py:17
  105.3 13.7 %collective-permute-start.10 = (f32[256,256]{1,0:T(8,128)S(1)}, f32[256,256]{1,0:T(8,128)S(1)}, u32[]{:S(2)}, u32[]{:S(2)}) collective-permute-start(f32[256,256]{1,0:T(8,128)S(1)} %get-tuple-element.31), channel_id=1, source_target_pairs={{4,0},{8,4},{12,8},{16,12},{20,16},{24,20},{28,24},{32,28},{36,32}... | collective-permute-start | bytes 786440 | tf_op jit(solution)/shard_map/ppermute | solution.py:17
  111.5 10.1 %collective-permute-start.11 = (f32[2,256,128]{2,1,0:T(8,128)S(1)}, f32[2,256,128]{2,1,0:T(8,128)S(1)}, u32[]{:S(2)}, u32[]{:S(2)}) collective-permute-start(f32[2,256,128]{2,1,0:T(8,128)S(1)} %get-tuple-element.36), channel_id=1, source_target_pairs={{1,0},{2,1},{3,2},{5,4},{6,5},{7,6},{9,8},{10,9},{11,10},{13,12},{... | collective-permute-start | bytes 786440 | tf_op jit(solution)/shard_map/ppermute | solution.py:17
  112.8 9.7 %collective-permute-start.13 = (f32[2,256,128]{2,1,0:T(8,128)S(1)}, f32[2,256,128]{2,1,0:T(8,128)S(1)}, u32[]{:S(2)}, u32[]{:S(2)}) collective-permute-start(f32[2,256,128]{2,1,0:T(8,128)S(1)} %get-tuple-element.35), channel_id=1, source_target_pairs={{0,1},{1,2},{2,3},{4,5},{5,6},{6,7},{8,9},{9,10},{10,11},{12,13},{... | collective-permute-start | bytes 786440 | tf_op jit(solution)/shard_map/ppermute | solution.py:17
  117.1 6.0 %collective-permute-start.12 = (f32[256,256]{1,0:T(8,128)S(1)}, f32[256,256]{1,0:T(8,128)S(1)}, u32[]{:S(2)}, u32[]{:S(2)}) collective-permute-start(f32[256,256]{1,0:T(8,128)S(1)} %get-tuple-element.30), channel_id=1, source_target_pairs={{0,4},{4,8},{8,12},{12,16},{16,20},{20,24},{24,28},{28,32},{32,36}... | collective-permute-start | bytes 786440 | tf_op jit(solution)/shard_map/ppermute | solution.py:17
  125.1 7.7 %collective-permute-start.14 = (f32[256,256]{1,0:T(8,128)S(1)}, f32[256,256]{1,0:T(8,128)S(1)}, u32[]{:S(2)}, u32[]{:S(2)}) collective-permute-start(f32[256,256]{1,0:T(8,128)S(1)} %get-tuple-element.27), channel_id=1, source_target_pairs={{4,0},{8,4},{12,8},{16,12},{20,16},{24,20},{28,24},{32,28},{36,32}... | collective-permute-start | bytes 786440 | tf_op jit(solution)/shard_map/ppermute | solution.py:17
  131.3 10.0 %collective-permute-start.15 = (f32[2,256,128]{2,1,0:T(8,128)S(1)}, f32[2,256,128]{2,1,0:T(8,128)S(1)}, u32[]{:S(2)}, u32[]{:S(2)}) collective-permute-start(f32[2,256,128]{2,1,0:T(8,128)S(1)} %slice.266), channel_id=1, source_target_pairs={{1,0},{2,1},{3,2},{5,4},{6,5},{7,6},{9,8},{10,9},{11,10},{13,12},{... | collective-permute-start | bytes 786440 | tf_op jit(solution)/shard_map/ppermute | solution.py:17
  132.7 8.7 %copy-start.1 = (f32[2,1,256,384]{3,2,1,0:T(8,128)S(1)}, f32[2,1,256,384]{3,2,1,0:T(8,128)}, u32[]{:S(2)}) copy-start(f32[2,1,256,384]{3,2,1,0:T(8,128)} %param.8) | copy-start | bytes 2359300

commit v3 on v2

--- a/solution.py
+++ b/solution.py
@@ -1,6 +1,10 @@
+from functools import partial
+
 import jax
 import jax.numpy as jnp
 from jax import lax
+from jax.experimental import pallas as pl
+from jax.experimental.pallas import tpu as pltpu
 from jax.sharding import PartitionSpec as P
 
 NB = 6
@@ -15,6 +19,47 @@
     count = lax.axis_size(axis)
     initial, last = (max(0, -steps), min(count, count - steps))
     return lax.ppermute(value, axis, [(source, source + steps) for source in range(initial, last)])
+
+
+def _gather_kernel(table_ref, tiles_ref, out_ref, *, rows, cols, block_len):
+    for r in range(rows):
+        for c in range(cols):
+            entry = r * cols + c
+            index = table_ref[0, entry]
+            mode = table_ref[1, entry]
+            rs = slice(r * block_len, (r + 1) * block_len)
+            cs = slice(c * block_len, (c + 1) * block_len)
+
+            @pl.when(mode == 0)
+            def _():
+                out_ref[rs, cs] = jnp.zeros((block_len, block_len), out_ref.dtype)
+
+            @pl.when(mode == 1)
+            def _():
+                out_ref[rs, cs] = tiles_ref[index]
+
+            @pl.when(mode == 2)
+            def _():
+                out_ref[rs, cs] = tiles_ref[index].astype(jnp.float32).T.astype(out_ref.dtype)
+
+
+def gather_tiles(table, tiles, rows, cols):
+    block_len = tiles.shape[-1]
+    count = tiles.shape[0]
+    kernel = partial(_gather_kernel, rows=rows, cols=cols, block_len=block_len)
+    size = 2 * block_len * block_len
+    return pl.pallas_call(
+        kernel,
+        out_shape=jax.ShapeDtypeStruct((rows * block_len, cols * block_len), tiles.dtype),
+        in_specs=[
+            pl.BlockSpec(memory_space=pltpu.SMEM),
+            pl.BlockSpec(memory_space=pltpu.VMEM),
+        ],
+        out_specs=pl.BlockSpec(memory_space=pltpu.VMEM),
+        cost_estimate=pl.CostEstimate(
+            flops=0, transcendentals=0, bytes_accessed=(count + rows * cols) * size
+        ),
+    )(table, tiles)
 
 
 def face_mask(counts, block_len):
@@ -81,12 +126,10 @@
     slot_rank = jnp.sum(same_owner.astype(jnp.int32), axis=1)
     send_slot = jnp.where(is_valid & (slot_rank < slot_cap), owner_gx * slot_cap + slot_rank, -1)
     slot_count = gx_count * slot_cap
-    pick_send = (
-        send_slot[None, :] == jnp.arange(slot_count, dtype=jnp.int32)[:, None]
-    ).astype(jnp.bfloat16)
-    send_tiles = jnp.einsum(
-        "mj,jab->mab", pick_send, tiles, preferred_element_type=jnp.float32
-    ).astype(jnp.bfloat16)
+    send_hit = send_slot[None, :] == jnp.arange(slot_count, dtype=jnp.int32)[:, None]
+    send_from = jnp.sum(jnp.where(send_hit, job_order[None, :], 0), axis=1)
+    send_mode = jnp.any(send_hit, axis=1).astype(jnp.int32)
+    send_tiles = gather_tiles(jnp.stack([send_from, send_mode]), tiles, slot_count, 1)
     send_tiles = send_tiles.reshape(gx_count, slot_cap * block_len, block_len)
     got_tiles = lax.all_to_all(send_tiles, "gx", split_axis=0, concat_axis=0, tiled=True)
     got_tiles = got_tiles.reshape(slot_count, block_len, block_len)
@@ -102,16 +145,19 @@
     local_number = tile_number - first_tile_own[0]
     got_slot = tile_number % gx_count * slot_cap + local_number // gx_count
     both_alive = alive[:, :, None] & alive[:, None, :]
-    slot_ids = jnp.arange(slot_count, dtype=jnp.int32)
-    hits = got_slot[..., None] == slot_ids
-    pick_upper = (hits & (both_alive & (row_slot <= col_slot))[..., None]).astype(jnp.bfloat16)
-    pick_lower = (hits & (both_alive & (row_slot > col_slot))[..., None]).astype(jnp.bfloat16)
-    matrices = jnp.einsum(
-        "spqf,fab->spaqb", pick_upper, got_tiles, preferred_element_type=jnp.float32
-    ) + jnp.einsum(
-        "spqf,fba->spaqb", pick_lower, got_tiles, preferred_element_type=jnp.float32
-    )
-    matrices = matrices.astype(jnp.bfloat16).reshape(sub_count, NB * block_len, NB * block_len)
+    matrix_mode = jnp.where(both_alive, jnp.where(row_slot <= col_slot, 1, 2), 0)
+    matrix_from = jnp.where(both_alive, jnp.clip(got_slot, 0, slot_count - 1), 0)
+    matrices = jnp.stack(
+        [
+            gather_tiles(
+                jnp.stack([matrix_from[sub].reshape(-1), matrix_mode[sub].reshape(-1)]),
+                got_tiles,
+                NB,
+                NB,
+            )
+            for sub in range(sub_count)
+        ]
+    )
 
     residual = dual_rhs[:, 0] * face_mask(counts, block_len)[:, None, :]
     cases = residual.shape[1]

time: 144 us -> 147 us (1.021); the launches traced: 143 us -> 144 us
  Pallas kernels: 0 us -> 11.2 us
  starting transfers between devices: 61.7 us -> 53.1 us
  local copies, waits for them, and re-layouts: 18.9 us -> 10.8 us
  waiting for transfers between devices: 30.3 us -> 36.2 us
  other arithmetic: 11.6 us -> 15 us
  matrix products: 19.2 us -> 16.6 us
    pallas_call x0 -> x3, Pallas kernels: none -> 11.2 us  [gather_tiles(): pl.pallas_call(kernel, out_shape=jax.ShapeDtypeStruct((rows * block_len,...]
    ppermute x16, starting transfers between devices: 53.8 us -> 45.3 us  [from_behind(): lax.ppermute(value, axis, [(source, source + steps) for source in range(i...]
    reshape x2 -> x0, local copies, waits for them, and re-layouts: 7.9 us -> none  [the longest x1 5 us: shards(): matrices.astype(jnp.bfloat16)]
    ppermute x16, waiting for transfers between devices: 30.3 us -> 36.2 us  [from_behind(): lax.ppermute(value, axis, [(source, source + steps) for source in range(i...]
    convert_element_type x2 -> x0, local copies, waits for them, and re-layouts: 5.09 us -> none  [the longest x1 2.71 us: shards(): send_tiles = jnp.einsum('mj,jab->mab', pick_send, tiles, preferred_elemen...]
    dot_general x3 -> x0, matrix products: 3.65 us -> none  [the longest x1 1.71 us: shards(): jnp.einsum('spqf,fab->spaqb', pick_upper, got_tiles, preferred_element_ty...]
    unnamed x14 -> x18, local copies, waits for them, and re-layouts: 0.03 us -> 2.41 us
    another operation x2 -> x5, other arithmetic: 0.2 us -> 1.97 us  [the longest x2 1.2 us: shards(): jnp.stack([matrix_from[sub].reshape(-1), matrix_mode[sub].reshape(-1)])]
  transfers between devices with their start and end apart: 17 -> 17, of which waited for: 9 -> 9; matrix products, arithmetic and copies ran while one was open for 8% -> 11% of each run, Pallas kernels for 0% -> 0%
where the time goes in v3:
time: 147 us; the launch traced here: 144 us
  starting transfers between devices  53.1 us (36%)
  waiting for transfers between devices  36.2 us (25%)
  matrix products  16.6 us (11%)
  other arithmetic  15 us (10%)
  Pallas kernels  11.2 us (8%)
  local copies, waits for them, and re-layouts  10.8 us (7%)
    ppermute x16, starting transfers between devices, from_behind(): lax.ppermute(value, axis, [(source, source + steps) for source in range(i...  45.3 us
    ppermute x16, waiting for transfers between devices, from_behind(): lax.ppermute(value, axis, [(source, source + steps) for source in range(i...  36.2 us
    pallas_call x3, Pallas kernels, gather_tiles(): pl.pallas_call(kernel, out_shape=jax.ShapeDtypeStruct((rows * block_len,...  11.2 us
    dot_general x1, matrix products, shards(): jnp.einsum('jka,jkb->jab', factor_panels[:, 0, 0], factor_panels[:, 0, 1]...  9.52 us
    all_to_all x1, starting transfers between devices, shards(): lax.all_to_all(send_tiles, 'gx', split_axis=0, concat_axis=0, tiled=True)  7.84 us
    dot_general x4, matrix products, shards(): jnp.einsum('ncm,nmk->nck', jnp.concatenate([high, low], axis=1), matrices...  7.12 us
  transfers between devices with their start and end apart: 17, of which 9 were waited for; matrix products, arithmetic and copies ran while one was open for 11% of the time, Pallas kernels for 0%

profile of v3, /device:TPU:17, one launch (start us, length us, event | category | flops | bytes accessed | tf_op | source)
XLA Modules:
  0.0 144.2 jit_solution(2304887012894005343)
XLA Ops:
  3.7 9.5 %fusion.25.tiles_ref = bf16[26,128,128]{2,1,0:T(8,128)(2,1)} fusion(bf16[26,1,2,1536,128]{4,3,2,1,0:T(8,128)(2,1)} %param.7), kind=kOutput, calls=%fused_computation.42 | convolution fusion | flops 1309048832 | bytes 21299200 | tf_op jit(solution)/shard_map/jka,jkb->jab/dot_general | solution.py:109
  13.8 3.8 %shard_map.68 = bf16[8192,128]{1,0:T(8,128)(2,1)} custom-call(s32[2,64]{1,0:T(2,128)} %pad_add_fusion.1.table_ref, bf16[26,128,128]{2,1,0:T(8,128)(2,1)} %fusion.25.tiles_ref), custom_call_target="tpu_custom_call" | custom-call | bytes 2949120 | tf_op jit(solution)/shard_map/pallas_call | solution.py:51
  17.5 7.8 %all-to-all-start = ((bf16[32,256,128]{2,1,0:T(8,128)(2,1)}), bf16[32,256,128]{2,1,0:T(8,128)(2,1)S(1)}, u32[]{:S(2)}, u32[]{:S(2)}) async-start(bf16[32,256,128]{2,1,0:T(8,128)(2,1)} %bitcast.136), calls=%async_computation | async-start | bytes 4194304 | tf_op jit(solution)/shard_map/all_to_all | solution.py:134
  26.1 2.1 %broadcast_multiply_fusion = (f32[2,256,384]{2,1,0:T(8,128)}, f32[2,256,384]{2,1,0:T(8,128)S(1)}) fusion(f32[2,384]{1,0:T(2,128)S(1)} %pad_convert_fusion, f32[2,1,256,384]{3,2,1,0:T(8,128)} %param.8), kind=kLoop, calls=%fused_computation.67 | loop fusion | flops 393216 | bytes 2362368 | tf_op jit(solution)/shard_map/div | solution.py:170
  28.9 3.4 %collective-permute-start = (f32[256,256]{1,0:T(8,128)}, f32[256,256]{1,0:T(8,128)S(1)}, u32[]{:S(2)}, u32[]{:S(2)}) collective-permute-start(f32[256,256]{1,0:T(8,128)} %slice_bitcast_fusion.7), channel_id=1, source_target_pairs={{0,4},{4,8},{8,12},{12,16},{16,20},{20,24},{24,28},{28,32},{32,36}... | collective-permute-start | bytes 786440 | tf_op jit(solution)/shard_map/ppermute | solution.py:21
  33.0 3.5 %collective-permute-start.1 = (f32[2,256,128]{2,1,0:T(8,128)}, f32[2,256,128]{2,1,0:T(8,128)S(1)}, u32[]{:S(2)}, u32[]{:S(2)}) collective-permute-start(f32[2,256,128]{2,1,0:T(8,128)} %slice.241), channel_id=1, source_target_pairs={{0,1},{1,2},{2,3},{4,5},{5,6},{6,7},{8,9},{9,10},{10,11},{12,13},{... | collective-permute-start | bytes 786440 | tf_op jit(solution)/shard_map/ppermute | solution.py:21
  37.5 1.7 %slice.242 = f32[2,256,128]{2,1,0:T(8,128)} slice(f32[2,256,384]{2,1,0:T(8,128)} %get-tuple-element.22), slice={[0:2], [0:256], [256:384]} | slice | bytes 524288 | tf_op jit(solution)/shard_map/slice | solution.py:177
  39.2 1.7 %slice.239 = f32[1,256,256]{2,1,0:T(8,128)} slice(f32[2,256,384]{2,1,0:T(8,128)} %get-tuple-element.22), slice={[0:1], [0:256], [0:256]} | slice | bytes 524288 | tf_op jit(solution)/shard_map/slice | solution.py:178
  40.8 1.9 %slice.240 = f32[2,256,256]{2,1,0:T(8,128)} slice(f32[2,256,384]{2,1,0:T(8,128)} %get-tuple-element.22), slice={[0:2], [0:256], [0:256]} | slice | bytes 1048576 | tf_op jit(solution)/shard_map/slice | solution.py:176
  44.2 8.1 %collective-permute-done = f32[256,256]{1,0:T(8,128)S(1)} collective-permute-done((f32[256,256]{1,0:T(8,128)}, f32[256,256]{1,0:T(8,128)S(1)}, u32[]{:S(2)}, u32[]{:S(2)}) %collective-permute-start) | collective-permute-done | bytes 262176 | tf_op jit(solution)/shard_map/ppermute | solution.py:21
  56.1 3.6 %shard_map.70 = bf16[768,768]{1,0:T(8,128)(2,1)} custom-call(s32[2,36]{1,0:T(2,128)} %pad_add_fusion.2.table_ref, bf16[64,128,128]{2,1,0:T(8,128)(2,1)} %bitcast.134), custom_call_target="tpu_custom_call" | custom-call | bytes 3276800 | tf_op jit(solution)/shard_map/pallas_call | solution.py:51
  59.8 3.8 %shard_map.69 = bf16[768,768]{1,0:T(8,128)(2,1)} custom-call(s32[2,36]{1,0:T(2,128)} %pad_add_fusion.table_ref, bf16[64,128,128]{2,1,0:T(8,128)(2,1)} %bitcast.135), custom_call_target="tpu_custom_call" | custom-call | bytes 3276800 | tf_op jit(solution)/shard_map/pallas_call | solution.py:51
  63.5 2.9 %fusion.9 = f32[2,512,768]{2,1,0:T(8,128)S(1)} fusion(bf16[2,256,768]{2,1,0:T(8,128)(2,1)} %get-tuple-element.54, bf16[2,256,768]{2,1,0:T(8,128)(2,1)S(1)} %copy-done.6, bf16[1,768,768]{2,1,0:T(8,128)(2,1)S(1)} %bitcast.141, bf16[1,768,768]{2,1,0:T(8,128)(2,1)} %bitcast.145), kind=kOutput, calls=%fused_computation.23 | convolution fusion | flops 1212284928 | bytes 7077888 | tf_op jit(solution)/shard_map/ncm,nmk->nck/dot_general | solution.py:183
  66.7 4.4 %collective-permute-start.2 = (f32[256,256]{1,0:T(8,128)S(1)}, f32[256,256]{1,0:T(8,128)S(1)}, u32[]{:S(2)}, u32[]{:S(2)}) collective-permute-start(f32[256,256]{1,0:T(8,128)S(1)} %get-tuple-element.48), channel_id=1, source_target_pairs={{4,0},{8,4},{12,8},{16,12},{20,16},{24,20},{28,24},{32,28},{36,32}... | collective-permute-start | bytes 786440 | tf_op jit(solution)/shard_map/ppermute | solution.py:21
  71.1 4.3 %collective-permute-start.5 = (f32[2,256,128]{2,1,0:T(8,128)S(1)}, f32[2,256,128]{2,1,0:T(8,128)S(1)}, u32[]{:S(2)}, u32[]{:S(2)}) collective-permute-start(f32[2,256,128]{2,1,0:T(8,128)S(1)} %get-tuple-element.51), channel_id=1, source_target_pairs={{0,1},{1,2},{2,3},{4,5},{5,6},{6,7},{8,9},{9,10},{10,11},{12,13},{... | collective-permute-start | bytes 786440 | tf_op jit(solution)/shard_map/ppermute | solution.py:21
  76.7 2.1 %collective-permute-start.4 = (f32[256,256]{1,0:T(8,128)S(1)}, f32[256,256]{1,0:T(8,128)S(1)}, u32[]{:S(2)}, u32[]{:S(2)}) collective-permute-start(f32[256,256]{1,0:T(8,128)S(1)} %get-tuple-element.47), channel_id=1, source_target_pairs={{0,4},{4,8},{8,12},{12,16},{16,20},{20,24},{24,28},{28,32},{32,36}... | collective-permute-start | bytes 786440 | tf_op jit(solution)/shard_map/ppermute | solution.py:21
  78.9 1.9 %collective-permute-done.5 = f32[2,256,128]{2,1,0:T(8,128)S(1)} collective-permute-done((f32[2,256,128]{2,1,0:T(8,128)S(1)}, f32[2,256,128]{2,1,0:T(8,128)S(1)}, u32[]{:S(2)}, u32[]{:S(2)}) %collective-permute-start.5) | collective-permute-done | bytes 262176 | tf_op jit(solution)/shard_map/ppermute | solution.py:21
  80.9 4.4 %collective-permute-done.3 = f32[2,256,128]{2,1,0:T(8,128)S(1)} collective-permute-done((f32[2,256,128]{2,1,0:T(8,128)S(1)}, f32[2,256,128]{2,1,0:T(8,128)S(1)}, u32[]{:S(2)}, u32[]{:S(2)}) %collective-permute-start.3) | collective-permute-done | bytes 262176 | tf_op jit(solution)/shard_map/ppermute | solution.py:21
  88.7 3.1 %collective-permute-start.6 = (f32[256,256]{1,0:T(8,128)S(1)}, f32[256,256]{1,0:T(8,128)S(1)}, u32[]{:S(2)}, u32[]{:S(2)}) collective-permute-start(f32[256,256]{1,0:T(8,128)S(1)} %get-tuple-element.40), channel_id=1, source_target_pairs={{4,0},{8,4},{12,8},{16,12},{20,16},{24,20},{28,24},{32,28},{36,32}... | collective-permute-start | bytes 786440 | tf_op jit(solution)/shard_map/ppermute | solution.py:21
  91.8 4.3 %collective-permute-start.9 = (f32[2,256,128]{2,1,0:T(8,128)S(1)}, f32[2,256,128]{2,1,0:T(8,128)S(1)}, u32[]{:S(2)}, u32[]{:S(2)}) collective-permute-start(f32[2,256,128]{2,1,0:T(8,128)S(1)} %get-tuple-element.43), channel_id=1, source_target_pairs={{0,1},{1,2},{2,3},{4,5},{5,6},{6,7},{8,9},{9,10},{10,11},{12,13},{... | collective-permute-start | bytes 786440 | tf_op jit(solution)/shard_map/ppermute | solution.py:21
  97.4 1.9 %collective-permute-start.8 = (f32[256,256]{1,0:T(8,128)S(1)}, f32[256,256]{1,0:T(8,128)S(1)}, u32[]{:S(2)}, u32[]{:S(2)}) collective-permute-start(f32[256,256]{1,0:T(8,128)S(1)} %get-tuple-element.39), channel_id=1, source_target_pairs={{0,4},{4,8},{8,12},{12,16},{16,20},{20,24},{24,28},{28,32},{32,36}... | collective-permute-start | bytes 786440 | tf_op jit(solution)/shard_map/ppermute | solution.py:21
  99.4 2.0 %collective-permute-done.9 = f32[2,256,128]{2,1,0:T(8,128)S(1)} collective-permute-done((f32[2,256,128]{2,1,0:T(8,128)S(1)}, f32[2,256,128]{2,1,0:T(8,128)S(1)}, u32[]{:S(2)}, u32[]{:S(2)}) %collective-permute-start.9) | collective-permute-done | bytes 262176 | tf_op jit(solution)/shard_map/ppermute | solution.py:21
  101.5 4.2 %collective-permute-done.7 = f32[2,256,128]{2,1,0:T(8,128)S(1)} collective-permute-done((f32[2,256,128]{2,1,0:T(8,128)S(1)}, f32[2,256,128]{2,1,0:T(8,128)S(1)}, u32[]{:S(2)}, u32[]{:S(2)}) %collective-permute-start.7) | collective-permute-done | bytes 262176 | tf_op jit(solution)/shard_map/ppermute | solution.py:21
  108.2 3.6 %collective-permute-start.10 = (f32[256,256]{1,0:T(8,128)S(1)}, f32[256,256]{1,0:T(8,128)S(1)}, u32[]{:S(2)}, u32[]{:S(2)}) collective-permute-start(f32[256,256]{1,0:T(8,128)S(1)} %get-tuple-element.31), channel_id=1, source_target_pairs={{4,0},{8,4},{12,8},{16,12},{20,16},{24,20},{28,24},{32,28},{36,32}... | collective-permute-start | bytes 786440 | tf_op jit(solution)/shard_map/ppermute | solution.py:21
  111.8 4.3 %collective-permute-start.13 = (f32[2,256,128]{2,1,0:T(8,128)S(1)}, f32[2,256,128]{2,1,0:T(8,128)S(1)}, u32[]{:S(2)}, u32[]{:S(2)}) collective-permute-start(f32[2,256,128]{2,1,0:T(8,128)S(1)} %get-tuple-element.35), channel_id=1, source_target_pairs={{0,1},{1,2},{2,3},{4,5},{5,6},{6,7},{8,9},{9,10},{10,11},{12,13},{... | collective-permute-start | bytes 786440 | tf_op jit(solution)/shard_map/ppermute | solution.py:21
  117.5 1.9 %collective-permute-start.12 = (f32[256,256]{1,0:T(8,128)S(1)}, f32[256,256]{1,0:T(8,128)S(1)}, u32[]{:S(2)}, u32[]{:S(2)}) collective-permute-start(f32[256,256]{1,0:T(8,128)S(1)} %get-tuple-element.30), channel_id=1, source_target_pairs={{0,4},{4,8},{8,12},{12,16},{16,20},{20,24},{24,28},{28,32},{32,36}... | collective-permute-start | bytes 786440 | tf_op jit(solution)/shard_map/ppermute | solution.py:21
  119.5 2.2 %collective-permute-done.13 = f32[2,256,128]{2,1,0:T(8,128)S(1)} collective-permute-done((f32[2,256,128]{2,1,0:T(8,128)S(1)}, f32[2,256,128]{2,1,0:T(8,128)S(1)}, u32[]{:S(2)}, u32[]{:S(2)}) %collective-permute-start.13) | collective-permute-done | bytes 262176 | tf_op jit(solution)/shard_map/ppermute | solution.py:21
  121.7 3.8 %collective-permute-done.11 = f32[2,256,128]{2,1,0:T(8,128)S(1)} collective-permute-done((f32[2,256,128]{2,1,0:T(8,128)S(1)}, f32[2,256,128]{2,1,0:T(8,128)S(1)}, u32[]{:S(2)}, u32[]{:S(2)}) %collective-permute-start.11) | collective-permute-done | bytes 262176 | tf_op jit(solution)/shard_map/ppermute | solution.py:21
  128.1 3.4 %collective-permute-start.14 = (f32[256,256]{1,0:T(8,128)S(1)}, f32[256,256]{1,0:T(8,128)S(1)}, u32[]{:S(2)}, u32[]{:S(2)}) collective-permute-start(f32[256,256]{1,0:T(8,128)S(1)} %get-tuple-element.27), channel_id=1, source_target_pairs={{4,0},{8,4},{12,8},{16,12},{20,16},{24,20},{28,24},{32,28},{36,32}... | collective-permute-start | bytes 786440 | tf_op jit(solution)/shard_map/ppermute | solution.py:21
  133.0 2.8 %collective-permute-done.14 = f32[256,256]{1,0:T(8,128)S(1)} collective-permute-done((f32[256,256]{1,0:T(8,128)S(1)}, f32[256,256]{1,0:T(8,128)S(1)}, u32[]{:S(2)}, u32[]{:S(2)}) %collective-permute-start.14) | collective-permute-done | bytes 262176 | tf_op jit(solution)/shard_map/ppermute | solution.py:21
  135.9 6.6 %collective-permute-done.15 = f32[2,256,128]{2,1,0:T(8,128)S(1)} collective-permute-done((f32[2,256,128]{2,1,0:T(8,128)S(1)}, f32[2,256,128]{2,1,0:T(8,128)S(1)}, u32[]{:S(2)}, u32[]{:S(2)}) %collective-permute-start.15) | collective-permute-done | bytes 262176 | tf_op jit(solution)/shard_map/ppermute | solution.py:21
  142.6 1.6 %fusion.32 = (f32[2,1,256,384]{3,2,1,0:T(8,128)}, f32[2,1,256,384]{3,2,1,0:T(8,128)}) fusion(f32[2,1,256,128]{3,2,0,1:T(8,128)S(1)} %fusion.34, f32[2,1,256,256]{3,2,0,1:T(8,128)S(1)} %fusion.33, f32[2,1,256,128]{3,2,0,1:T(8,128)S(1)} %bitcast.140, f32[2,1,256,256]{3,2,0,1:T(8,128)S(1)} %fusion.77, f32[2,1,256,128]{3,2,0,1:T(8,128)S(1)} %bitcast.139, ...), kind=kLoop, calls=%fused_computation.52 | loop fusion | flops 4325376 | bytes 5508096
  (123 shorter events, 26.2 us)
Async XLA Ops:
  17.5 7.9 %copy-start.7 = (s32[64,1]{0,1:T(1,128)S(1)}, s32[64,1]{0,1:T(1,128)}, u32[]{:S(2)}) copy-start(s32[64,1]{0,1:T(1,128)} %param.5) | copy-start | bytes 772
  17.5 37.2 %all-to-all-start = ((bf16[32,256,128]{2,1,0:T(8,128)(2,1)}), bf16[32,256,128]{2,1,0:T(8,128)(2,1)S(1)}, u32[]{:S(2)}, u32[]{:S(2)}) async-start(bf16[32,256,128]{2,1,0:T(8,128)(2,1)} %bitcast.136), calls=%async_computation | async-start | bytes 4194304 | tf_op jit(solution)/shard_map/all_to_all | solution.py:134
  26.1 11.2 %copy-start.8 = (s32[6]{0:T(128)S(1)}, s32[6]{0:T(128)}, u32[]{:S(2)}) copy-start(s32[6]{0:T(128)} %constant.149.clone) | copy-start | bytes 76
  28.9 23.4 %collective-permute-start = (f32[256,256]{1,0:T(8,128)}, f32[256,256]{1,0:T(8,128)S(1)}, u32[]{:S(2)}, u32[]{:S(2)}) collective-permute-start(f32[256,256]{1,0:T(8,128)} %slice_bitcast_fusion.7), channel_id=1, source_target_pairs={{0,4},{4,8},{8,12},{12,16},{16,20},{20,24},{24,28},{28,32},{32,36}... | collective-permute-start | bytes 786440 | tf_op jit(solution)/shard_map/ppermute | solution.py:21
  33.0 20.3 %collective-permute-start.1 = (f32[2,256,128]{2,1,0:T(8,128)}, f32[2,256,128]{2,1,0:T(8,128)S(1)}, u32[]{:S(2)}, u32[]{:S(2)}) collective-permute-start(f32[2,256,128]{2,1,0:T(8,128)} %slice.241), channel_id=1, source_target_pairs={{0,1},{1,2},{2,3},{4,5},{5,6},{6,7},{8,9},{9,10},{10,11},{12,13},{... | collective-permute-start | bytes 786440 | tf_op jit(solution)/shard_map/ppermute | solution.py:21
  43.0 10.4 %copy-start.2 = (f32[2,256,256]{2,1,0:T(8,128)S(1)}, f32[2,256,256]{2,1,0:T(8,128)}, u32[]{:S(2)}) copy-start(f32[2,256,256]{2,1,0:T(8,128)} %slice.240) | copy-start | bytes 1572868
  43.0 10.4 %copy-start.5 = (f32[2,256,128]{2,1,0:T(8,128)S(1)}, f32[2,256,128]{2,1,0:T(8,128)}, u32[]{:S(2)}) copy-start(f32[2,256,128]{2,1,0:T(8,128)} %slice.242) | copy-start | bytes 786436
  54.8 1.4 copy-start
  59.8 3.8 %copy-start.3 = (bf16[768,768]{1,0:T(8,128)(2,1)S(1)}, bf16[768,768]{1,0:T(8,128)(2,1)}, u32[]{:S(2)}) copy-start(bf16[768,768]{1,0:T(8,128)(2,1)} %shard_map.70) | copy-start | bytes 3538948
  59.8 3.8 %copy-start.6 = (bf16[2,256,768]{2,1,0:T(8,128)(2,1)S(1)}, bf16[2,256,768]{2,1,0:T(8,128)(2,1)}, u32[]{:S(2)}) copy-start(bf16[2,256,768]{2,1,0:T(8,128)(2,1)} %get-tuple-element.53) | copy-start | bytes 2359300
  66.7 12.1 %collective-permute-start.2 = (f32[256,256]{1,0:T(8,128)S(1)}, f32[256,256]{1,0:T(8,128)S(1)}, u32[]{:S(2)}, u32[]{:S(2)}) collective-permute-start(f32[256,256]{1,0:T(8,128)S(1)} %get-tuple-element.48), channel_id=1, source_target_pairs={{4,0},{8,4},{12,8},{16,12},{20,16},{24,20},{28,24},{32,28},{36,32}... | collective-permute-start | bytes 786440 | tf_op jit(solution)/shard_map/ppermute | solution.py:21
  71.1 9.7 %collective-permute-start.5 = (f32[2,256,128]{2,1,0:T(8,128)S(1)}, f32[2,256,128]{2,1,0:T(8,128)S(1)}, u32[]{:S(2)}, u32[]{:S(2)}) collective-permute-start(f32[2,256,128]{2,1,0:T(8,128)S(1)} %get-tuple-element.51), channel_id=1, source_target_pairs={{0,1},{1,2},{2,3},{4,5},{5,6},{6,7},{8,9},{9,10},{10,11},{12,13},{... | collective-permute-start | bytes 786440 | tf_op jit(solution)/shard_map/ppermute | solution.py:21
  75.4 9.8 %collective-permute-start.3 = (f32[2,256,128]{2,1,0:T(8,128)S(1)}, f32[2,256,128]{2,1,0:T(8,128)S(1)}, u32[]{:S(2)}, u32[]{:S(2)}) collective-permute-start(f32[2,256,128]{2,1,0:T(8,128)S(1)} %get-tuple-element.52), channel_id=1, source_target_pairs={{1,0},{2,1},{3,2},{5,4},{6,5},{7,6},{9,8},{10,9},{11,10},{13,12},{... | collective-permute-start | bytes 786440 | tf_op jit(solution)/shard_map/ppermute | solution.py:21
  76.7 8.9 %collective-permute-start.4 = (f32[256,256]{1,0:T(8,128)S(1)}, f32[256,256]{1,0:T(8,128)S(1)}, u32[]{:S(2)}, u32[]{:S(2)}) collective-permute-start(f32[256,256]{1,0:T(8,128)S(1)} %get-tuple-element.47), channel_id=1, source_target_pairs={{0,4},{4,8},{8,12},{12,16},{16,20},{20,24},{24,28},{28,32},{32,36}... | collective-permute-start | bytes 786440 | tf_op jit(solution)/shard_map/ppermute | solution.py:21
  85.7 1.3 copy-start.4
  88.7 10.7 %collective-permute-start.6 = (f32[256,256]{1,0:T(8,128)S(1)}, f32[256,256]{1,0:T(8,128)S(1)}, u32[]{:S(2)}, u32[]{:S(2)}) collective-permute-start(f32[256,256]{1,0:T(8,128)S(1)} %get-tuple-element.40), channel_id=1, source_target_pairs={{4,0},{8,4},{12,8},{16,12},{20,16},{24,20},{28,24},{32,28},{36,32}... | collective-permute-start | bytes 786440 | tf_op jit(solution)/shard_map/ppermute | solution.py:21
  91.8 9.6 %collective-permute-start.9 = (f32[2,256,128]{2,1,0:T(8,128)S(1)}, f32[2,256,128]{2,1,0:T(8,128)S(1)}, u32[]{:S(2)}, u32[]{:S(2)}) collective-permute-start(f32[2,256,128]{2,1,0:T(8,128)S(1)} %get-tuple-element.43), channel_id=1, source_target_pairs={{0,1},{1,2},{2,3},{4,5},{5,6},{6,7},{8,9},{9,10},{10,11},{12,13},{... | collective-permute-start | bytes 786440 | tf_op jit(solution)/shard_map/ppermute | solution.py:21
  96.1 9.5 %collective-permute-start.7 = (f32[2,256,128]{2,1,0:T(8,128)S(1)}, f32[2,256,128]{2,1,0:T(8,128)S(1)}, u32[]{:S(2)}, u32[]{:S(2)}) collective-permute-start(f32[2,256,128]{2,1,0:T(8,128)S(1)} %get-tuple-element.44), channel_id=1, source_target_pairs={{1,0},{2,1},{3,2},{5,4},{6,5},{7,6},{9,8},{10,9},{11,10},{13,12},{... | collective-permute-start | bytes 786440 | tf_op jit(solution)/shard_map/ppermute | solution.py:21
  97.4 8.7 %collective-permute-start.8 = (f32[256,256]{1,0:T(8,128)S(1)}, f32[256,256]{1,0:T(8,128)S(1)}, u32[]{:S(2)}, u32[]{:S(2)}) collective-permute-start(f32[256,256]{1,0:T(8,128)S(1)} %get-tuple-element.39), channel_id=1, source_target_pairs={{0,4},{4,8},{8,12},{12,16},{16,20},{20,24},{24,28},{28,32},{32,36}... | collective-permute-start | bytes 786440 | tf_op jit(solution)/shard_map/ppermute | solution.py:21
  108.2 11.2 %collective-permute-start.10 = (f32[256,256]{1,0:T(8,128)S(1)}, f32[256,256]{1,0:T(8,128)S(1)}, u32[]{:S(2)}, u32[]{:S(2)}) collective-permute-start(f32[256,256]{1,0:T(8,128)S(1)} %get-tuple-element.31), channel_id=1, source_target_pairs={{4,0},{8,4},{12,8},{16,12},{20,16},{24,20},{28,24},{32,28},{36,32}... | collective-permute-start | bytes 786440 | tf_op jit(solution)/shard_map/ppermute | solution.py:21
  111.8 9.9 %collective-permute-start.13 = (f32[2,256,128]{2,1,0:T(8,128)S(1)}, f32[2,256,128]{2,1,0:T(8,128)S(1)}, u32[]{:S(2)}, u32[]{:S(2)}) collective-permute-start(f32[2,256,128]{2,1,0:T(8,128)S(1)} %get-tuple-element.35), channel_id=1, source_target_pairs={{0,1},{1,2},{2,3},{4,5},{5,6},{6,7},{8,9},{9,10},{10,11},{12,13},{... | collective-permute-start | bytes 786440 | tf_op jit(solution)/shard_map/ppermute | solution.py:21
  116.1 9.5 %collective-permute-start.11 = (f32[2,256,128]{2,1,0:T(8,128)S(1)}, f32[2,256,128]{2,1,0:T(8,128)S(1)}, u32[]{:S(2)}, u32[]{:S(2)}) collective-permute-start(f32[2,256,128]{2,1,0:T(8,128)S(1)} %get-tuple-element.36), channel_id=1, source_target_pairs={{1,0},{2,1},{3,2},{5,4},{6,5},{7,6},{9,8},{10,9},{11,10},{13,12},{... | collective-permute-start | bytes 786440 | tf_op jit(solution)/shard_map/ppermute | solution.py:21
  117.5 8.6 %collective-permute-start.12 = (f32[256,256]{1,0:T(8,128)S(1)}, f32[256,256]{1,0:T(8,128)S(1)}, u32[]{:S(2)}, u32[]{:S(2)}) collective-permute-start(f32[256,256]{1,0:T(8,128)S(1)} %get-tuple-element.30), channel_id=1, source_target_pairs={{0,4},{4,8},{8,12},{12,16},{16,20},{20,24},{24,28},{28,32},{32,36}... | collective-permute-start | bytes 786440 | tf_op jit(solution)/shard_map/ppermute | solution.py:21
  128.1 7.7 %collective-permute-start.14 = (f32[256,256]{1,0:T(8,128)S(1)}, f32[256,256]{1,0:T(8,128)S(1)}, u32[]{:S(2)}, u32[]{:S(2)}) collective-permute-start(f32[256,256]{1,0:T(8,128)S(1)} %get-tuple-element.27), channel_id=1, source_target_pairs={{4,0},{8,4},{12,8},{16,12},{20,16},{24,20},{28,24},{32,28},{36,32}... | collective-permute-start | bytes 786440 | tf_op jit(solution)/shard_map/ppermute | solution.py:21
  131.6 10.9 %collective-permute-start.15 = (f32[2,256,128]{2,1,0:T(8,128)S(1)}, f32[2,256,128]{2,1,0:T(8,128)S(1)}, u32[]{:S(2)}, u32[]{:S(2)}) collective-permute-start(f32[2,256,128]{2,1,0:T(8,128)S(1)} %slice.286), channel_id=1, source_target_pairs={{1,0},{2,1},{3,2},{5,4},{6,5},{7,6},{9,8},{10,9},{11,10},{13,12},{... | collective-permute-start | bytes 786440 | tf_op jit(solution)/shard_map/ppermute | solution.py:21
  133.0 9.6 %copy-start.1 = (f32[2,1,256,384]{3,2,1,0:T(8,128)S(1)}, f32[2,1,256,384]{3,2,1,0:T(8,128)}, u32[]{:S(2)}) copy-start(f32[2,1,256,384]{3,2,1,0:T(8,128)} %param.8) | copy-start | bytes 2359300
